TPU v7x, 32 devices: a whole 2x2x4 slice. The times are simulated.
32 devices in a mesh: group: 2 (over y), ctx: 8 (over z, x), tsp: 2 (over core).
Axes of the slice: x: 2, y: 2, z: 4, core: 2. Of those that a mesh axis runs over, the one named last changes fastest.
Arguments:
- query_proj: bfloat16 [4096, 2048], P(('group', 'ctx'), 'tsp'), parts along dimension 0, may hold values from -8 to 8
- key_proj: bfloat16 [4096, 1024], P(('group', 'ctx'), 'tsp'), parts along dimension 0, may hold values from -8 to 8
- value_projection: bfloat16 [4096, 1024], P(('group', 'ctx'), 'tsp'), parts along dimension 0, may hold values from -6 to 6
- grad_out: bfloat16 [4096, 2048], P(('group', 'ctx', 'tsp')), parts along dimension 0, may hold values from -6 to 6
- doc_ids: int32 [4096], P(('group', 'ctx')), parts along dimension 0, may hold values from 0 to 3, never falling along the last dimension, each value on 1 to 1024 neighbouring positions
- advantages: float32 [8], P('group'), parts along dimension 0, may hold values from -4 to 4
- head_window: int32 [16], P('tsp'), may hold values from 512 to 1024, as said below
Outputs:
- query_grad: bfloat16 [4096, 2048], P(('group', 'ctx'), 'tsp'), parts along dimension 0
- key_grad: bfloat16 [4096, 1024], P(('group', 'ctx'), 'tsp'), parts along dimension 0
- value_grad: bfloat16 [4096, 1024], P(('group', 'ctx'), 'tsp'), parts along dimension 0
There are 2 independent parts, one for each index of `group`. A program takes and returns all parts, laid end to end along the dimension named above; an argument that names none is the same for every part. Nothing has to cross between parts.
Inputs may be any that keep to these rules, and one draw needn't show every extreme that they name: `doc_ids`: document numbers never fall along the sequence; every document holds 1 to 1024 positions. `head_window`: some head has a window of exactly 1024.
All inputs are finite; a program needn't handle non-finite values.
Results may differ from a plain program's by a relative error of at most 0.039.
Values may be sent and summed in bfloat16 or wider, within the bound.
No kernel may reach another device: no remote copies, remote signals or barrier semaphores. Data moves between devices by JAX's collectives and lax.ppermute only.
A program may use at most 64 MiB of HBM per device.

v0:
```python
import jax
import jax.numpy as jnp
from jax import lax
from jax.sharding import PartitionSpec as P

HEAD_DIMENSION = 128
WINDOW = 1024


score_scale = 168.0 ** (-0.5)


def passed_along(value, axis, steps):
    count = lax.axis_size(axis)
    initial, last = (max(0, -steps), min(count, count - steps))
    return lax.ppermute(value, axis, [(source, source + steps) for source in range(initial, last)])


def head_grads(operands, query_pos, key_pos, doc_start):
    query_row_block, key_rows, value_rows, grad_rows, windows = operands
    row_count = query_row_block.shape[0]
    group_size = windows.shape[0]
    head_size = key_rows.shape[1]
    query_three = query_row_block.reshape(row_count, group_size, head_size)
    grad_three = grad_rows.reshape(row_count, group_size, head_size)
    scores = (
        jnp.einsum("rgd,sd->grs", query_three, key_rows, preferred_element_type=jnp.float32)
        * score_scale
    )
    offset = query_pos[:, None] - key_pos[None, :]
    allowed = (offset >= 0) & (key_pos[None, :] >= doc_start[:, None])
    live = allowed[None, :, :] & (offset[None, :, :] < windows[:, None, None])
    scores = jnp.where(live, scores, jnp.float32(-1e30))
    top = jnp.max(scores, axis=-1, keepdims=True)
    prob = jnp.exp(scores - top)
    prob = prob / jnp.sum(prob, axis=-1, keepdims=True)
    prob_low = prob.astype(jnp.bfloat16)
    attended = jnp.einsum(
        "grs,sd->rgd", prob_low, value_rows, preferred_element_type=jnp.float32
    ).astype(jnp.bfloat16)
    delta = jnp.sum(grad_three.astype(jnp.float32) * attended.astype(jnp.float32), axis=-1).T
    dprob = jnp.einsum("rgd,sd->grs", grad_three, value_rows, preferred_element_type=jnp.float32)
    dscore = (prob * (dprob - delta[:, :, None])).astype(jnp.bfloat16)
    query_part = (
        jnp.einsum("grs,sd->rgd", dscore, key_rows, preferred_element_type=jnp.float32)
        * score_scale
    )
    key_segment_slice = (
        jnp.einsum("grs,rgd->sd", dscore, query_three, preferred_element_type=jnp.float32)
        * score_scale
    )
    value_part = jnp.einsum("grs,rgd->sd", prob_low, grad_three, preferred_element_type=jnp.float32)
    return (
        query_part.reshape(row_count, group_size * head_size).astype(jnp.bfloat16),
        key_segment_slice,
        value_part,
    )


def on_device(query_proj, key_proj, value_projection, grad_out, doc_ids, advantages, head_window):
    tok_rows = query_proj.shape[0]
    kv_heads = key_proj.shape[1] // HEAD_DIMENSION
    q_heads = query_proj.shape[1] // HEAD_DIMENSION
    group_size = q_heads // kv_heads
    blocks = WINDOW // tok_rows
    seq_len = tok_rows * lax.axis_size("ctx")
    first_pos = lax.axis_index("ctx") * tok_rows
    positions = first_pos + jnp.arange(tok_rows, dtype=jnp.int32)
    doc_count = advantages.shape[0]
    matches = doc_ids[:, None] == jnp.arange(doc_count, dtype=jnp.int32)[None, :]
    local_first = jnp.min(jnp.where(matches, positions[:, None], jnp.int32(seq_len)), axis=0)
    doc_first = lax.pmin(local_first, "ctx")
    doc_start = jnp.max(jnp.where(matches, doc_first[None, :], jnp.int32(0)), axis=1)
    token_weight = jnp.sum(jnp.where(matches, advantages[None, :], jnp.float32(0.0)), axis=1)
    grad_local = lax.all_to_all(grad_out, "tsp", split_axis=1, concat_axis=0, tiled=True)
    weighted = (token_weight[:, None] * grad_local.astype(jnp.float32)).astype(jnp.bfloat16)
    paired = jnp.concatenate([key_proj, value_projection], axis=1)
    earlier = [passed_along(paired, "ctx", distance) for distance in range(blocks, 0, -1)]
    paired_all = jnp.concatenate(earlier + [paired], axis=0)
    query_stack = query_proj.reshape(tok_rows, kv_heads, group_size * HEAD_DIMENSION).transpose(
        1, 0, 2
    )
    grad_stack = weighted.reshape(tok_rows, kv_heads, group_size * HEAD_DIMENSION).transpose(
        1, 0, 2
    )
    window_stack = head_window.reshape(kv_heads, group_size)
    key_width = kv_heads * HEAD_DIMENSION
    key_count = paired_all.shape[0]
    key_pos = first_pos - (blocks - 0) * tok_rows + jnp.arange(key_count, dtype=jnp.int32)
    key_stack = (
        paired_all[:, :key_width].reshape(key_count, kv_heads, HEAD_DIMENSION).transpose(1, 0, 2)
    )
    value_stack = (
        paired_all[:, key_width:].reshape(key_count, kv_heads, HEAD_DIMENSION).transpose(1, 0, 2)
    )
    results = lax.map(
        lambda operands: head_grads(operands, positions, key_pos, doc_start),
        (query_stack, key_stack, value_stack, grad_stack, window_stack),
    )
    query_block = results[0].transpose(1, 0, 2).reshape(tok_rows, q_heads * HEAD_DIMENSION)
    key_block = results[1].transpose(1, 0, 2).reshape(key_count, key_width)
    value_block = results[2].transpose(1, 0, 2).reshape(key_count, key_width)
    filler = jnp.zeros((0 * tok_rows, 2 * key_width), jnp.float32)
    pair_grads = jnp.concatenate(
        [filler, jnp.concatenate([key_block, value_block], axis=1)], axis=0
    )
    query_grad, pair_grads = (query_block, pair_grads)
    own_part = pair_grads[blocks * tok_rows :]
    cross_low = pair_grads[: blocks * tok_rows].astype(jnp.bfloat16)
    summed = own_part
    for distance in range(1, blocks + 1):
        piece = cross_low[(blocks - distance) * tok_rows : (blocks - distance + 1) * tok_rows]
        arrived = passed_along(piece, "ctx", -distance)
        summed = summed + arrived.astype(jnp.float32)
    key_grad = summed[:, :key_width].astype(jnp.bfloat16)
    value_grad = summed[:, key_width:].astype(jnp.bfloat16)
    return (query_grad, key_grad, value_grad)


def solution(mesh):
    in_specs = (
        P(("group", "ctx"), "tsp"),
        P(("group", "ctx"), "tsp"),
        P(("group", "ctx"), "tsp"),
        P(("group", "ctx", "tsp"), None),
        P(("group", "ctx")),
        P("group"),
        P("tsp"),
    )
    out_specs = (P(("group", "ctx"), "tsp"), P(("group", "ctx"), "tsp"), P(("group", "ctx"), "tsp"))
    return jax.shard_map(
        on_device, mesh=mesh, in_specs=in_specs, out_specs=out_specs, check_vma=False
    )
```

profile of v0, /device:TPU:8, one launch (start us, length us, event | category | flops | bytes accessed | tf_op | source)
XLA Modules:
  0.0 230.2 jit_solution(9727675742280614129)
XLA Ops:
  0.7 1.1 copy.44
  1.8 1.1 copy.45
  2.8 0.8 pad_maximum_fusion
  3.7 3.4 %collective-permute-start.3 = (bf16[256,1024]{0,1:T(8,128)(2,1)}, bf16[256,1024]{0,1:T(8,128)(2,1)}, u32[]{:S(2)}, u32[]{:S(2)}) collective-permute-start(bf16[256,1024]{0,1:T(8,128)(2,1)} %pad_maximum_fusion), channel_id=1, source_target_pairs={{0,2},{2,4},{4,6},{6,8},{8,10},{10,12},{12,14},{1,3},{3,5},{5,7},{... | collective-permute-start | bytes 1572872 | tf_op jit(solution)/shard_map/ppermute | solution.py:16
  7.1 3.5 %collective-permute-start.2 = (bf16[256,1024]{0,1:T(8,128)(2,1)}, bf16[256,1024]{0,1:T(8,128)(2,1)}, u32[]{:S(2)}, u32[]{:S(2)}) collective-permute-start(bf16[256,1024]{0,1:T(8,128)(2,1)} %pad_maximum_fusion), channel_id=1, source_target_pairs={{0,4},{2,6},{4,8},{6,10},{8,12},{10,14},{1,5},{3,7},{5,9},{7,11},{... | collective-permute-start | bytes 1572872 | tf_op jit(solution)/shard_map/ppermute | solution.py:16
  10.6 3.7 %collective-permute-start.1 = (bf16[256,1024]{0,1:T(8,128)(2,1)}, bf16[256,1024]{0,1:T(8,128)(2,1)}, u32[]{:S(2)}, u32[]{:S(2)}) collective-permute-start(bf16[256,1024]{0,1:T(8,128)(2,1)} %pad_maximum_fusion), channel_id=1, source_target_pairs={{0,6},{2,8},{4,10},{6,12},{8,14},{1,7},{3,9},{5,11},{7,13},{9,15},... | collective-permute-start | bytes 1572872 | tf_op jit(solution)/shard_map/ppermute | solution.py:16
  14.3 2.1 collective-permute-start
  16.4 1.9 copy.73
  18.3 3.5 %all-to-all-start = ((bf16[128,2,1024]{2,0,1:T(8,128)(2,1)}), bf16[128,2,1024]{2,0,1:T(8,128)(2,1)S(1)}, u32[]{:S(2)}, u32[]{:S(2)}) async-start(bf16[128,2,1024]{2,0,1:T(8,128)(2,1)} %bitcast.130), calls=%async_computation | async-start | bytes 1048576 | tf_op jit(solution)/shard_map/all_to_all | solution.py:75
  21.9 1.6 all-to-all-done
  23.7 0.5 reshape.155
  24.6 31.1 %pmin.7 = s32[4]{0:T(128)S(1)} all-reduce(s32[4]{0:T(128)S(1)} %select_reduce_fusion.2), channel_id=1, replica_groups=mesh['group'=2,'ctx'=8,'tsp'=2] {'ctx'}, use_global_device_ids=true, to_apply=%region_2.3 | all-reduce | flops 4 | bytes 32 | tf_op jit(solution)/shard_map/pmin | solution.py:72
  55.7 1.0 copy.46
  56.8 1.1 copy.50
  58.0 1.1 constant_dynamic-update-slice_fusion.5
  59.1 1.1 constant_dynamic-update-slice_fusion.4
  60.2 1.1 constant_dynamic-update-slice_fusion.3
  61.3 1.1 constant_dynamic-update-slice_fusion.2
  62.4 1.7 fusion.63
  64.1 68.3 %while.15 = (s32[]{:T(128)}, bf16[4,256,256]{1,2,0:T(8,128)(2,1)}, f32[4,1280,128]{2,1,0:T(8,128)}, f32[4,1280,128]{2,1,0:T(8,128)}, bf16[4,1280,128]{1,2,0:T(8,...) while((s32[]{:T(128)}, bf16[4,256,256]{1,2,0:T(8,128)(2,1)}, ...), condition=%wide.region_8.9_spmd.clone, body=%wide.region_4.8_spmd.clone.sunk | while | flops 1360172800 | bytes 20874448 | solution.py:96
  64.1 1.0 constant_dynamic-slice_fusion.4
  65.8 3.7 %fusion.115 = (f32[2,256]{1,0:T(2,128)S(1)}, f32[2,256,1280]{1,2,0:T(8,128)}) fusion(bf16[256,2,128]{0,2,1:T(8,128)(2,1)S(1)} %bitcast.185, s32[256,1280]{0,1:T(8,128)S(1)} %broadcast_subtract_fusion.2, s32[2]{0:T(128)S(1)} %fusion.114, pred[256,1280]{0,1:T(8,128)(4,1)S(1)} %compare_and_fusion.2, bf16[4,1280,128]{1,2,0:T(8,128)(2,1)} %get-tuple-element.270, ...), kind=kOutput, calls=%fused_computation.74.clone.1 | convolution fusion | flops 171705600 | bytes 4720652 | tf_op jit(solution)/shard_map/while/body/eval_jaxpr/sub | solution.py:35
  69.5 2.6 %fusion.116 = f32[256,2]{0,1:T(2,128)S(1)} fusion(bf16[4,1280,128]{1,2,0:T(8,128)(2,1)} %get-tuple-element.274, s32[]{:T(128)S(6)} %copy.85, bf16[256,2,128]{0,2,1:T(8,128)(2,1)S(1)} %bitcast.190, f32[2,256]{1,0:T(2,128)S(1)} %get-tuple-element.238, bf16[256,2,128]{0,2,1:T(8,128)(2,1)S(1)} %bitcast.186, ...), kind=kOutput, calls=%fused_computation.26.clone.1 | convolution fusion | flops 340460800 | bytes 2561032 | tf_op jit(solution)/shard_map/while/body/eval_jaxpr/grs,sd->rgd/dot_general | solution.py:38
  72.1 2.4 %fusion.117 = bf16[2,256,1280]{1,2,0:T(8,128)(2,1)S(1)} fusion(bf16[256,2,128]{0,2,1:T(8,128)(2,1)S(1)} %bitcast.191, f32[2,256]{1,0:T(2,128)S(1)} %bitcast.194, f32[2,256,1280]{1,2,0:T(8,128)} %get-tuple-element.239, f32[2,256]{1,0:T(2,128)S(1)} %get-tuple-element.238, bf16[4,1280,128]{1,2,0:T(8,128)(2,1)} %get-tuple-element.274, s32[]{:T(128)S(6)} %copy.85), kind=kOutput, calls=%fused_computation.11.clone.1 | convolution fusion | flops 170393600 | bytes 4395012 | tf_op jit(solution)/shard_map/while/body/eval_jaxpr/rgd,sd->grs/dot_general | solution.py:42
  74.5 1.3 fusion.118
  75.8 0.7 constant_dynamic-update-slice_fusion.7
  76.5 3.4 %fusion.120 = f32[4,1280,128]{2,1,0:T(8,128)} fusion(f32[4,1280,128]{2,1,0:T(8,128)} %get-tuple-element.256, s32[]{:T(128)S(6)} %copy.85, bf16[256,2,128]{0,2,1:T(8,128)(2,1)S(1)} %bitcast.192, f32[2,256]{1,0:T(2,128)S(1)} %get-tuple-element.238, bf16[256,2,128]{0,2,1:T(8,128)(2,1)S(1)} %bitcast.187, s32[256,1280]{0,1:T(8,128)S(1)} %broadcast_subtract_fusion.2, ...), kind=kOutput, calls=%fused_computation.13.clone.1 | convolution fusion | flops 340133632 | bytes 2886664 | tf_op jit(solution)/shard_map/while/body/eval_jaxpr/grs,rgd->sd/dot_general | solution.py:52
  79.8 1.3 fusion.119
  81.2 1.0 constant_dynamic-slice_fusion.4
  82.8 3.7 %fusion.115 = (f32[2,256]{1,0:T(2,128)S(1)}, f32[2,256,1280]{1,2,0:T(8,128)}) fusion(bf16[256,2,128]{0,2,1:T(8,128)(2,1)S(1)} %bitcast.185, s32[256,1280]{0,1:T(8,128)S(1)} %broadcast_subtract_fusion.2, s32[2]{0:T(128)S(1)} %fusion.114, pred[256,1280]{0,1:T(8,128)(4,1)S(1)} %compare_and_fusion.2, bf16[4,1280,128]{1,2,0:T(8,128)(2,1)} %get-tuple-element.270, ...), kind=kOutput, calls=%fused_computation.74.clone.1 | convolution fusion | flops 171705600 | bytes 4720652 | tf_op jit(solution)/shard_map/while/body/eval_jaxpr/sub | solution.py:35
  86.5 2.6 %fusion.116 = f32[256,2]{0,1:T(2,128)S(1)} fusion(bf16[4,1280,128]{1,2,0:T(8,128)(2,1)} %get-tuple-element.274, s32[]{:T(128)S(6)} %copy.85, bf16[256,2,128]{0,2,1:T(8,128)(2,1)S(1)} %bitcast.190, f32[2,256]{1,0:T(2,128)S(1)} %get-tuple-element.238, bf16[256,2,128]{0,2,1:T(8,128)(2,1)S(1)} %bitcast.186, ...), kind=kOutput, calls=%fused_computation.26.clone.1 | convolution fusion | flops 340460800 | bytes 2561032 | tf_op jit(solution)/shard_map/while/body/eval_jaxpr/grs,sd->rgd/dot_general | solution.py:38
  89.1 2.4 %fusion.117 = bf16[2,256,1280]{1,2,0:T(8,128)(2,1)S(1)} fusion(bf16[256,2,128]{0,2,1:T(8,128)(2,1)S(1)} %bitcast.191, f32[2,256]{1,0:T(2,128)S(1)} %bitcast.194, f32[2,256,1280]{1,2,0:T(8,128)} %get-tuple-element.239, f32[2,256]{1,0:T(2,128)S(1)} %get-tuple-element.238, bf16[4,1280,128]{1,2,0:T(8,128)(2,1)} %get-tuple-element.274, s32[]{:T(128)S(6)} %copy.85), kind=kOutput, calls=%fused_computation.11.clone.1 | convolution fusion | flops 170393600 | bytes 4395012 | tf_op jit(solution)/shard_map/while/body/eval_jaxpr/rgd,sd->grs/dot_general | solution.py:42
  91.5 1.3 fusion.118
  92.9 0.7 constant_dynamic-update-slice_fusion.7
  93.5 3.4 %fusion.120 = f32[4,1280,128]{2,1,0:T(8,128)} fusion(f32[4,1280,128]{2,1,0:T(8,128)} %get-tuple-element.256, s32[]{:T(128)S(6)} %copy.85, bf16[256,2,128]{0,2,1:T(8,128)(2,1)S(1)} %bitcast.192, f32[2,256]{1,0:T(2,128)S(1)} %get-tuple-element.238, bf16[256,2,128]{0,2,1:T(8,128)(2,1)S(1)} %bitcast.187, s32[256,1280]{0,1:T(8,128)S(1)} %broadcast_subtract_fusion.2, ...), kind=kOutput, calls=%fused_computation.13.clone.1 | convolution fusion | flops 340133632 | bytes 2886664 | tf_op jit(solution)/shard_map/while/body/eval_jaxpr/grs,rgd->sd/dot_general | solution.py:52
  96.9 1.4 fusion.119
  98.3 1.0 constant_dynamic-slice_fusion.4
  99.9 3.7 %fusion.115 = (f32[2,256]{1,0:T(2,128)S(1)}, f32[2,256,1280]{1,2,0:T(8,128)}) fusion(bf16[256,2,128]{0,2,1:T(8,128)(2,1)S(1)} %bitcast.185, s32[256,1280]{0,1:T(8,128)S(1)} %broadcast_subtract_fusion.2, s32[2]{0:T(128)S(1)} %fusion.114, pred[256,1280]{0,1:T(8,128)(4,1)S(1)} %compare_and_fusion.2, bf16[4,1280,128]{1,2,0:T(8,128)(2,1)} %get-tuple-element.270, ...), kind=kOutput, calls=%fused_computation.74.clone.1 | convolution fusion | flops 171705600 | bytes 4720652 | tf_op jit(solution)/shard_map/while/body/eval_jaxpr/sub | solution.py:35
  103.6 2.6 %fusion.116 = f32[256,2]{0,1:T(2,128)S(1)} fusion(bf16[4,1280,128]{1,2,0:T(8,128)(2,1)} %get-tuple-element.274, s32[]{:T(128)S(6)} %copy.85, bf16[256,2,128]{0,2,1:T(8,128)(2,1)S(1)} %bitcast.190, f32[2,256]{1,0:T(2,128)S(1)} %get-tuple-element.238, bf16[256,2,128]{0,2,1:T(8,128)(2,1)S(1)} %bitcast.186, ...), kind=kOutput, calls=%fused_computation.26.clone.1 | convolution fusion | flops 340460800 | bytes 2561032 | tf_op jit(solution)/shard_map/while/body/eval_jaxpr/grs,sd->rgd/dot_general | solution.py:38
  106.2 2.4 %fusion.117 = bf16[2,256,1280]{1,2,0:T(8,128)(2,1)S(1)} fusion(bf16[256,2,128]{0,2,1:T(8,128)(2,1)S(1)} %bitcast.191, f32[2,256]{1,0:T(2,128)S(1)} %bitcast.194, f32[2,256,1280]{1,2,0:T(8,128)} %get-tuple-element.239, f32[2,256]{1,0:T(2,128)S(1)} %get-tuple-element.238, bf16[4,1280,128]{1,2,0:T(8,128)(2,1)} %get-tuple-element.274, s32[]{:T(128)S(6)} %copy.85), kind=kOutput, calls=%fused_computation.11.clone.1 | convolution fusion | flops 170393600 | bytes 4395012 | tf_op jit(solution)/shard_map/while/body/eval_jaxpr/rgd,sd->grs/dot_general | solution.py:42
  108.6 1.3 fusion.118
  109.9 0.7 constant_dynamic-update-slice_fusion.7
  110.6 3.4 %fusion.120 = f32[4,1280,128]{2,1,0:T(8,128)} fusion(f32[4,1280,128]{2,1,0:T(8,128)} %get-tuple-element.256, s32[]{:T(128)S(6)} %copy.85, bf16[256,2,128]{0,2,1:T(8,128)(2,1)S(1)} %bitcast.192, f32[2,256]{1,0:T(2,128)S(1)} %get-tuple-element.238, bf16[256,2,128]{0,2,1:T(8,128)(2,1)S(1)} %bitcast.187, s32[256,1280]{0,1:T(8,128)S(1)} %broadcast_subtract_fusion.2, ...), kind=kOutput, calls=%fused_computation.13.clone.1 | convolution fusion | flops 340133632 | bytes 2886664 | tf_op jit(solution)/shard_map/while/body/eval_jaxpr/grs,rgd->sd/dot_general | solution.py:52
  113.9 1.4 fusion.119
  115.3 1.0 constant_dynamic-slice_fusion.4
  117.0 3.7 %fusion.115 = (f32[2,256]{1,0:T(2,128)S(1)}, f32[2,256,1280]{1,2,0:T(8,128)}) fusion(bf16[256,2,128]{0,2,1:T(8,128)(2,1)S(1)} %bitcast.185, s32[256,1280]{0,1:T(8,128)S(1)} %broadcast_subtract_fusion.2, s32[2]{0:T(128)S(1)} %fusion.114, pred[256,1280]{0,1:T(8,128)(4,1)S(1)} %compare_and_fusion.2, bf16[4,1280,128]{1,2,0:T(8,128)(2,1)} %get-tuple-element.270, ...), kind=kOutput, calls=%fused_computation.74.clone.1 | convolution fusion | flops 171705600 | bytes 4720652 | tf_op jit(solution)/shard_map/while/body/eval_jaxpr/sub | solution.py:35
  120.7 2.6 %fusion.116 = f32[256,2]{0,1:T(2,128)S(1)} fusion(bf16[4,1280,128]{1,2,0:T(8,128)(2,1)} %get-tuple-element.274, s32[]{:T(128)S(6)} %copy.85, bf16[256,2,128]{0,2,1:T(8,128)(2,1)S(1)} %bitcast.190, f32[2,256]{1,0:T(2,128)S(1)} %get-tuple-element.238, bf16[256,2,128]{0,2,1:T(8,128)(2,1)S(1)} %bitcast.186, ...), kind=kOutput, calls=%fused_computation.26.clone.1 | convolution fusion | flops 340460800 | bytes 2561032 | tf_op jit(solution)/shard_map/while/body/eval_jaxpr/grs,sd->rgd/dot_general | solution.py:38
  123.3 2.4 %fusion.117 = bf16[2,256,1280]{1,2,0:T(8,128)(2,1)S(1)} fusion(bf16[256,2,128]{0,2,1:T(8,128)(2,1)S(1)} %bitcast.191, f32[2,256]{1,0:T(2,128)S(1)} %bitcast.194, f32[2,256,1280]{1,2,0:T(8,128)} %get-tuple-element.239, f32[2,256]{1,0:T(2,128)S(1)} %get-tuple-element.238, bf16[4,1280,128]{1,2,0:T(8,128)(2,1)} %get-tuple-element.274, s32[]{:T(128)S(6)} %copy.85), kind=kOutput, calls=%fused_computation.11.clone.1 | convolution fusion | flops 170393600 | bytes 4395012 | tf_op jit(solution)/shard_map/while/body/eval_jaxpr/rgd,sd->grs/dot_general | solution.py:42
  125.7 1.3 fusion.118
  127.0 0.7 constant_dynamic-update-slice_fusion.7
  127.6 3.4 %fusion.120 = f32[4,1280,128]{2,1,0:T(8,128)} fusion(f32[4,1280,128]{2,1,0:T(8,128)} %get-tuple-element.256, s32[]{:T(128)S(6)} %copy.85, bf16[256,2,128]{0,2,1:T(8,128)(2,1)S(1)} %bitcast.192, f32[2,256]{1,0:T(2,128)S(1)} %get-tuple-element.238, bf16[256,2,128]{0,2,1:T(8,128)(2,1)S(1)} %bitcast.187, s32[256,1280]{0,1:T(8,128)S(1)} %broadcast_subtract_fusion.2, ...), kind=kOutput, calls=%fused_computation.13.clone.1 | convolution fusion | flops 340133632 | bytes 2886664 | tf_op jit(solution)/shard_map/while/body/eval_jaxpr/grs,rgd->sd/dot_general | solution.py:52
  131.0 1.3 fusion.119
  132.4 2.2 bitcast_dynamic-update-slice_fusion.1
  135.7 1.9 copy-done
  137.6 1.2 fusion.62
  138.8 1.9 collective-permute-start.4
  140.8 1.3 collective-permute-start.7
  142.1 1.3 collective-permute-start.6
  143.4 1.9 collective-permute-start.5
  145.3 2.0 copy.62
  147.3 28.7 %collective-permute-done.4 = bf16[256,1024]{1,0:T(8,128)(2,1)S(1)} collective-permute-done((bf16[256,1024]{1,0:T(8,128)(2,1)}, bf16[256,1024]{1,0:T(8,128)(2,1)S(1)}, u32[]{:S(2)}, u32[]{:S(2)}) %collective-permute-start.4) | collective-permute-done | bytes 524320 | tf_op jit(solution)/shard_map/ppermute | solution.py:16
  176.0 51.8 %collective-permute-done.5 = bf16[256,1024]{1,0:T(8,128)(2,1)S(1)} collective-permute-done((bf16[256,1024]{1,0:T(8,128)(2,1)S(1)}, bf16[256,1024]{1,0:T(8,128)(2,1)S(1)}, u32[]{:S(2)}, u32[]{:S(2)}) %collective-permute-start.5) | collective-permute-done | bytes 524320 | tf_op jit(solution)/shard_map/ppermute | solution.py:16
  227.8 1.6 fusion.57
  229.4 0.8 fusion.64
  (50 shorter events, 4.4 us)
Async XLA Ops:
  0.6 21.1 %copy-start.3 = (s32[256]{0:T(256)S(1)}, s32[256]{0:T(256)}, u32[]{:S(2)}) copy-start(s32[256]{0:T(256)} %param.13) | copy-start | bytes 3076
  0.6 21.1 %copy-start.4 = (f32[4]{0:T(128)S(1)}, f32[4]{0:T(128)}, u32[]{:S(2)}) copy-start(f32[4]{0:T(128)} %param.14) | copy-start | bytes 52
  3.7 57.6 %collective-permute-start.3 = (bf16[256,1024]{0,1:T(8,128)(2,1)}, bf16[256,1024]{0,1:T(8,128)(2,1)}, u32[]{:S(2)}, u32[]{:S(2)}) collective-permute-start(bf16[256,1024]{0,1:T(8,128)(2,1)} %pad_maximum_fusion), channel_id=1, source_target_pairs={{0,2},{2,4},{4,6},{6,8},{8,10},{10,12},{12,14},{1,3},{3,5},{5,7},{... | collective-permute-start | bytes 1572872 | tf_op jit(solution)/shard_map/ppermute | solution.py:16
  7.1 53.1 %collective-permute-start.2 = (bf16[256,1024]{0,1:T(8,128)(2,1)}, bf16[256,1024]{0,1:T(8,128)(2,1)}, u32[]{:S(2)}, u32[]{:S(2)}) collective-permute-start(bf16[256,1024]{0,1:T(8,128)(2,1)} %pad_maximum_fusion), channel_id=1, source_target_pairs={{0,4},{2,6},{4,8},{6,10},{8,12},{10,14},{1,5},{3,7},{5,9},{7,11},{... | collective-permute-start | bytes 1572872 | tf_op jit(solution)/shard_map/ppermute | solution.py:16
  10.6 48.5 %collective-permute-start.1 = (bf16[256,1024]{0,1:T(8,128)(2,1)}, bf16[256,1024]{0,1:T(8,128)(2,1)}, u32[]{:S(2)}, u32[]{:S(2)}) collective-permute-start(bf16[256,1024]{0,1:T(8,128)(2,1)} %pad_maximum_fusion), channel_id=1, source_target_pairs={{0,6},{2,8},{4,10},{6,12},{8,14},{1,7},{3,9},{5,11},{7,13},{9,15},... | collective-permute-start | bytes 1572872 | tf_op jit(solution)/shard_map/ppermute | solution.py:16
  14.3 43.7 %collective-permute-start = (bf16[256,1024]{0,1:T(8,128)(2,1)}, bf16[256,1024]{0,1:T(8,128)(2,1)}, u32[]{:S(2)}, u32[]{:S(2)}) collective-permute-start(bf16[256,1024]{0,1:T(8,128)(2,1)} %pad_maximum_fusion), channel_id=1, source_target_pairs={{0,8},{2,10},{4,12},{6,14},{1,9},{3,11},{5,13},{7,15},{16,24},{18,... | collective-permute-start | bytes 1572872 | tf_op jit(solution)/shard_map/ppermute | solution.py:16
  18.3 5.2 %all-to-all-start = ((bf16[128,2,1024]{2,0,1:T(8,128)(2,1)}), bf16[128,2,1024]{2,0,1:T(8,128)(2,1)S(1)}, u32[]{:S(2)}, u32[]{:S(2)}) async-start(bf16[128,2,1024]{2,0,1:T(8,128)(2,1)} %bitcast.130), calls=%async_computation | async-start | bytes 1048576 | tf_op jit(solution)/shard_map/all_to_all | solution.py:75
  21.9 33.8 %copy-start.5 = (s32[8]{0:T(128)S(1)}, s32[8]{0:T(128)}, u32[]{:S(2)}) copy-start(s32[8]{0:T(128)} %param.15) | copy-start | bytes 100
  21.9 33.9 %copy-start.2 = (bf16[256,1024]{1,0:T(8,128)(2,1)S(1)}, bf16[256,1024]{1,0:T(8,128)(2,1)}, u32[]{:S(2)}) copy-start(bf16[256,1024]{1,0:T(8,128)(2,1)} %param.9) | copy-start | bytes 1572868
  132.4 2.5 %copy-start.1 = (f32[4,1280,128]{2,1,0:T(8,128)S(1)}, f32[4,1280,128]{2,1,0:T(8,128)}, u32[]{:S(2)}) copy-start(f32[4,1280,128]{2,1,0:T(8,128)} %get-tuple-element.69) | copy-start | bytes 7864324
  135.3 2.3 %copy-start = (f32[1280,1024]{1,0:T(8,128)}, f32[1280,1024]{1,0:T(8,128)S(1)}, u32[]{:S(2)}) copy-start(f32[1280,1024]{1,0:T(8,128)S(1)} %bitcast_dynamic-update-slice_fusion) | copy-start | bytes 15728644
  138.8 37.1 %collective-permute-start.4 = (bf16[256,1024]{1,0:T(8,128)(2,1)}, bf16[256,1024]{1,0:T(8,128)(2,1)S(1)}, u32[]{:S(2)}, u32[]{:S(2)}) collective-permute-start(bf16[256,1024]{1,0:T(8,128)(2,1)} %get-tuple-element.151), channel_id=1, source_target_pairs={{2,0},{4,2},{6,4},{8,6},{10,8},{12,10},{14,12},{3,1},{5,3},{7,5},{... | collective-permute-start | bytes 1572872 | tf_op jit(solution)/shard_map/ppermute | solution.py:16
  140.8 35.2 %collective-permute-start.7 = (bf16[256,1024]{1,0:T(8,128)(2,1)}, bf16[256,1024]{1,0:T(8,128)(2,1)S(1)}, u32[]{:S(2)}, u32[]{:S(2)}) collective-permute-start(bf16[256,1024]{1,0:T(8,128)(2,1)} %get-tuple-element.152), channel_id=1, source_target_pairs={{8,0},{10,2},{12,4},{14,6},{9,1},{11,3},{13,5},{15,7},{24,16},{26,... | collective-permute-start | bytes 1572872 | tf_op jit(solution)/shard_map/ppermute | solution.py:16
  142.1 33.9 %collective-permute-start.6 = (bf16[256,1024]{1,0:T(8,128)(2,1)S(1)}, bf16[256,1024]{1,0:T(8,128)(2,1)S(1)}, u32[]{:S(2)}, u32[]{:S(2)}) collective-permute-start(bf16[256,1024]{1,0:T(8,128)(2,1)S(1)} %get-tuple-element.153), channel_id=1, source_target_pairs={{6,0},{8,2},{10,4},{12,6},{14,8},{7,1},{9,3},{11,5},{13,7},{15,9},... | collective-permute-start | bytes 1572872 | tf_op jit(solution)/shard_map/ppermute | solution.py:16
  143.4 84.4 %collective-permute-start.5 = (bf16[256,1024]{1,0:T(8,128)(2,1)S(1)}, bf16[256,1024]{1,0:T(8,128)(2,1)S(1)}, u32[]{:S(2)}, u32[]{:S(2)}) collective-permute-start(bf16[256,1024]{1,0:T(8,128)(2,1)S(1)} %get-tuple-element.154), channel_id=1, source_target_pairs={{4,0},{6,2},{8,4},{10,6},{12,8},{14,10},{5,1},{7,3},{9,5},{11,7},{... | collective-permute-start | bytes 1572872 | tf_op jit(solution)/shard_map/ppermute | solution.py:16
where the time goes:
time: 232 us; the launch traced here: 230 us
  waiting for transfers between devices  82.1 us (35%)
  matrix products  59 us (25%)
  blocking collectives  31.1 us (13%)
  local copies, waits for them, and re-layouts  28.4 us (12%)
  starting transfers between devices  22.6 us (10%)
  other arithmetic  6.09 us (3%)
    ppermute x8, waiting for transfers between devices, passed_along(): lax.ppermute(value, axis, [(source, source + steps) for source in range(i...  80.4 us
    pmin x1, blocking collectives, on_device(): doc_first = lax.pmin(local_first, 'ctx')  31.1 us
    ppermute x8, starting transfers between devices, passed_along(): lax.ppermute(value, axis, [(source, source + steps) for source in range(i...  19.1 us
    sub x4, matrix products, head_grads(): prob = jnp.exp(scores - top)  14.8 us
    dot_general x4, matrix products, head_grads(): jnp.einsum('grs,rgd->sd', prob_low, grad_three, preferred_element_type=jn...  13.5 us
    unnamed x21, local copies, waits for them, and re-layouts  13.1 us
    dot_general x4, matrix products, head_grads(): jnp.einsum('grs,sd->rgd', prob_low, value_rows, preferred_element_type=jn...  10.5 us
    dot_general x4, matrix products, head_grads(): jnp.einsum('rgd,sd->grs', grad_three, value_rows, preferred_element_type=...  9.55 us
  transfers between devices with their start and end apart: 9, of which 3 were waited for; matrix products, arithmetic and copies ran while one was open for 5% of the time, Pallas kernels for 0%

commit v1 on v0

v1 whole, which is shorter than its diff:
```python
import jax
import jax.numpy as jnp
from jax import lax
from jax.sharding import PartitionSpec as P

HEAD_DIMENSION = 128
WINDOW = 1024
KV_PER_CHUNK = 1


score_scale = 168.0 ** (-0.5)


def passed_along(value, axis, steps):
    count = lax.axis_size(axis)
    initial, last = (max(0, -steps), min(count, count - steps))
    return lax.ppermute(value, axis, [(source, source + steps) for source in range(initial, last)])


def head_grads(query_row_block, key_rows, value_rows, grad_rows, windows, base_live, offset):
    row_count = query_row_block.shape[0]
    group_size = windows.shape[0]
    head_size = key_rows.shape[1]
    query_three = query_row_block.reshape(row_count, group_size, head_size)
    grad_three = grad_rows.reshape(row_count, group_size, head_size)
    scores = (
        jnp.einsum("rgd,sd->grs", query_three, key_rows, preferred_element_type=jnp.float32)
        * score_scale
    )
    live = base_live[None, :, :] & (offset[None, :, :] < windows[:, None, None])
    scores = jnp.where(live, scores, jnp.float32(-1e30))
    top = jnp.max(scores, axis=-1, keepdims=True)
    prob = jnp.exp(scores - top)
    prob = prob / jnp.sum(prob, axis=-1, keepdims=True)
    prob_low = prob.astype(jnp.bfloat16)
    attended = jnp.einsum(
        "grs,sd->rgd", prob_low, value_rows, preferred_element_type=jnp.float32
    ).astype(jnp.bfloat16)
    delta = jnp.sum(grad_three.astype(jnp.float32) * attended.astype(jnp.float32), axis=-1).T
    dprob = jnp.einsum("rgd,sd->grs", grad_three, value_rows, preferred_element_type=jnp.float32)
    dscore = (prob * (dprob - delta[:, :, None])).astype(jnp.bfloat16)
    query_part = (
        jnp.einsum("grs,sd->rgd", dscore, key_rows, preferred_element_type=jnp.float32)
        * score_scale
    )
    key_part = (
        jnp.einsum("grs,rgd->sd", dscore, query_three, preferred_element_type=jnp.float32)
        * score_scale
    )
    value_part = jnp.einsum("grs,rgd->sd", prob_low, grad_three, preferred_element_type=jnp.float32)
    return (
        query_part.reshape(row_count, group_size * head_size).astype(jnp.bfloat16),
        key_part,
        value_part,
    )


def on_device(query_proj, key_proj, value_projection, grad_out, doc_ids, advantages, head_window):
    tok_rows = query_proj.shape[0]
    kv_heads = key_proj.shape[1] // HEAD_DIMENSION
    q_heads = query_proj.shape[1] // HEAD_DIMENSION
    group_size = q_heads // kv_heads
    blocks = WINDOW // tok_rows
    first_pos = lax.axis_index("ctx") * tok_rows
    positions = first_pos + jnp.arange(tok_rows, dtype=jnp.int32)
    doc_count = advantages.shape[0]
    matches = doc_ids[:, None] == jnp.arange(doc_count, dtype=jnp.int32)[None, :]
    token_weight = jnp.sum(jnp.where(matches, advantages[None, :], jnp.float32(0.0)), axis=1)
    grad_local = lax.all_to_all(grad_out, "tsp", split_axis=1, concat_axis=0, tiled=True)
    weighted = (token_weight[:, None] * grad_local.astype(jnp.float32)).astype(jnp.bfloat16)

    ids_earlier = [passed_along(doc_ids, "ctx", distance) for distance in range(blocks, 0, -1)]
    key_ids = jnp.concatenate(ids_earlier + [doc_ids], axis=0)
    key_count = key_ids.shape[0]
    key_pos = first_pos - blocks * tok_rows + jnp.arange(key_count, dtype=jnp.int32)
    offset = positions[:, None] - key_pos[None, :]
    base_live = (
        (offset >= 0) & (key_pos[None, :] >= 0) & (key_ids[None, :] == doc_ids[:, None])
    )

    chunk_heads = KV_PER_CHUNK
    chunk_count = kv_heads // chunk_heads
    chunk_width = chunk_heads * HEAD_DIMENSION
    query_width = group_size * HEAD_DIMENSION
    window_stack = head_window.reshape(kv_heads, group_size)

    query_pieces, key_pieces, value_pieces = [], [], []
    previous = None
    for chunk in range(chunk_count):
        cols = slice(chunk * chunk_width, (chunk + 1) * chunk_width)
        paired = jnp.concatenate([key_proj[:, cols], value_projection[:, cols]], axis=1)
        if previous is not None:
            paired, _ = lax.optimization_barrier((paired, previous))
        earlier = [passed_along(paired, "ctx", distance) for distance in range(blocks, 0, -1)]
        previous = earlier
        paired_all = jnp.concatenate(earlier + [paired], axis=0)
        key_grads, value_grads = [], []
        for inner in range(chunk_heads):
            head = chunk * chunk_heads + inner
            key_rows = paired_all[:, inner * HEAD_DIMENSION : (inner + 1) * HEAD_DIMENSION]
            value_rows = paired_all[
                :, chunk_width + inner * HEAD_DIMENSION : chunk_width + (inner + 1) * HEAD_DIMENSION
            ]
            qcols = slice(head * query_width, (head + 1) * query_width)
            query_part, key_part, value_part = head_grads(
                query_proj[:, qcols],
                key_rows,
                value_rows,
                weighted[:, qcols],
                window_stack[head],
                base_live,
                offset,
            )
            query_pieces.append(query_part)
            key_grads.append(key_part)
            value_grads.append(value_part)
        pair_grads = jnp.concatenate(key_grads + value_grads, axis=1)
        own_part = pair_grads[blocks * tok_rows :]
        cross_low = pair_grads[: blocks * tok_rows].astype(jnp.bfloat16)
        summed = own_part
        for distance in range(1, blocks + 1):
            piece = cross_low[(blocks - distance) * tok_rows : (blocks - distance + 1) * tok_rows]
            arrived = passed_along(piece, "ctx", -distance)
            summed = summed + arrived.astype(jnp.float32)
        key_pieces.append(summed[:, :chunk_width])
        value_pieces.append(summed[:, chunk_width:])
    query_grad = jnp.concatenate(query_pieces, axis=1)
    key_grad = jnp.concatenate(key_pieces, axis=1).astype(jnp.bfloat16)
    value_grad = jnp.concatenate(value_pieces, axis=1).astype(jnp.bfloat16)
    return (query_grad, key_grad, value_grad)


def solution(mesh):
    in_specs = (
        P(("group", "ctx"), "tsp"),
        P(("group", "ctx"), "tsp"),
        P(("group", "ctx"), "tsp"),
        P(("group", "ctx", "tsp"), None),
        P(("group", "ctx")),
        P("group"),
        P("tsp"),
    )
    out_specs = (P(("group", "ctx"), "tsp"), P(("group", "ctx"), "tsp"), P(("group", "ctx"), "tsp"))
    return jax.shard_map(
        on_device, mesh=mesh, in_specs=in_specs, out_specs=out_specs, check_vma=False
    )
```

time: 232 us -> 203 us (0.88)
  starting transfers between devices: 22.6 us -> 102 us
  waiting for transfers between devices: 82.1 us -> 17.7 us
  matrix products: 59 us -> 26.2 us
  blocking collectives: 31.1 us -> 0 us
  other arithmetic: 6.09 us -> 17.6 us
  local copies, waits for them, and re-layouts: 28.4 us -> 36 us
    ppermute x8 -> x36, starting transfers between devices: 19.1 us -> 98.4 us  [passed_along(): lax.ppermute(value, axis, [(source, source + steps) for source in range(i...]
    ppermute x8 -> x36, waiting for transfers between devices: 80.4 us -> 17.7 us  [passed_along(): lax.ppermute(value, axis, [(source, source + steps) for source in range(i...]
    pmin x1 -> x0, blocking collectives: 31.1 us -> none  [on_device(): doc_first = lax.pmin(local_first, 'ctx')]
    dot_general x4, matrix products: 13.5 us -> 3.17 us  [head_grads(): jnp.einsum('grs,rgd->sd', prob_low, grad_three, preferred_element_type=jn...]
    unnamed x21 -> x93, local copies, waits for them, and re-layouts: 13.1 us -> 23.2 us
    dot_general x4, matrix products: 10.5 us -> 1.53 us  [head_grads(): jnp.einsum('grs,sd->rgd', prob_low, value_rows, preferred_element_type=jn...]
    dot_general x4, matrix products: 9.55 us -> 1.95 us  [head_grads(): jnp.einsum('rgd,sd->grs', grad_three, value_rows, preferred_element_type=...]
    convert_element_type x0 -> x5, other arithmetic: none -> 6.24 us  [the longest x4 6.12 us: head_grads(): prob_low = prob.astype(jnp.bfloat16)]
  transfers between devices with their start and end apart: 9 -> 37, of which waited for: 3 -> 6; matrix products, arithmetic and copies ran while one was open for 5% -> 35% of each run, Pallas kernels for 0% -> 0%
where the time goes in v1:
time: 203 us; the launch traced here: 201 us
  starting transfers between devices  102 us (50%)
  local copies, waits for them, and re-layouts  36 us (18%)
  matrix products  26.2 us (13%)
  waiting for transfers between devices  17.7 us (9%)
  other arithmetic  17.6 us (9%)
    ppermute x36, starting transfers between devices, passed_along(): lax.ppermute(value, axis, [(source, source + steps) for source in range(i...  98.4 us
    unnamed x93, local copies, waits for them, and re-layouts  23.2 us
    ppermute x36, waiting for transfers between devices, passed_along(): lax.ppermute(value, axis, [(source, source + steps) for source in range(i...  17.7 us
    sub x4, matrix products, head_grads(): prob = jnp.exp(scores - top)  14.5 us
    convert_element_type x4, other arithmetic, head_grads(): prob_low = prob.astype(jnp.bfloat16)  6.12 us
    another operation x8, other arithmetic  4.84 us
    convert_element_type x4, local copies, waits for them, and re-layouts, head_grads(): query_part.reshape(row_count, group_size * head_size).astype(jnp.bfloat16)  4.19 us
  transfers between devices with their start and end apart: 37, of which 6 were waited for; matrix products, arithmetic and copies ran while one was open for 35% of the time, Pallas kernels for 0%

profile of v1, /device:TPU:8, one launch (start us, length us, event | category | flops | bytes accessed | tf_op | source)
XLA Modules:
  0.0 201.3 jit_solution(11778707123306796294)
XLA Ops:
  0.7 3.5 %collective-permute-start.7 = (s32[256]{0:T(256)}, s32[256]{0:T(256)S(1)}, u32[]{:S(2)}, u32[]{:S(2)}) collective-permute-start(s32[256]{0:T(256)} %param.11), channel_id=1, source_target_pairs={{0,2},{2,4},{4,6},{6,8},{8,10},{10,12},{12,14},{1,3},{3,5},{5,7},{... | collective-permute-start | bytes 3080 | tf_op jit(solution)/shard_map/ppermute | solution.py:17
  4.2 3.5 %collective-permute-start.6 = (s32[256]{0:T(256)}, s32[256]{0:T(256)S(1)}, u32[]{:S(2)}, u32[]{:S(2)}) collective-permute-start(s32[256]{0:T(256)} %param.11), channel_id=1, source_target_pairs={{0,4},{2,6},{4,8},{6,10},{8,12},{10,14},{1,5},{3,7},{5,9},{7,11},{... | collective-permute-start | bytes 3080 | tf_op jit(solution)/shard_map/ppermute | solution.py:17
  7.7 2.9 %collective-permute-start.5 = (s32[256]{0:T(256)}, s32[256]{0:T(256)S(1)}, u32[]{:S(2)}, u32[]{:S(2)}) collective-permute-start(s32[256]{0:T(256)} %param.11), channel_id=1, source_target_pairs={{0,6},{2,8},{4,10},{6,12},{8,14},{1,7},{3,9},{5,11},{7,13},{9,15},... | collective-permute-start | bytes 3080 | tf_op jit(solution)/shard_map/ppermute | solution.py:17
  10.6 1.3 collective-permute-start.4
  11.9 2.0 %copy.148 = bf16[128,2048]{0,1:T(8,128)(2,1)} copy(bf16[128,2048]{1,0:T(8,128)(2,1)} %param.10) | data formatting | bytes 1048576 | tf_op args[3]
  13.9 3.6 %all-to-all-start = ((bf16[128,2,1024]{0,2,1:T(8,128)(2,1)}), bf16[128,2,1024]{0,2,1:T(8,128)(2,1)S(1)}, u32[]{:S(2)}, u32[]{:S(2)}) async-start(bf16[128,2,1024]{0,2,1:T(8,128)(2,1)} %bitcast.5), calls=%async_computation | async-start | bytes 1048576 | tf_op jit(solution)/shard_map/all_to_all | solution.py:69
  17.7 2.8 %collective-permute-start.3 = (bf16[256,256]{1,0:T(8,128)(2,1)S(1)}, bf16[256,256]{1,0:T(8,128)(2,1)S(1)}, u32[]{:S(2)}, u32[]{:S(2)}) collective-permute-start(bf16[256,256]{1,0:T(8,128)(2,1)S(1)} %pad_maximum_fusion.7), channel_id=1, source_target_pairs={{0,2},{2,4},{4,6},{6,8},{8,10},{10,12},{12,14},{1,3},{3,5},{5,7},{... | collective-permute-start | bytes 393224 | tf_op jit(solution)/shard_map/ppermute | solution.py:17
  24.7 1.3 broadcast_subtract_fusion
  30.2 1.9 collective-permute-start.2
  32.2 1.3 collective-permute-start.1
  33.5 1.3 collective-permute-start
  34.9 2.1 %compare_and_fusion = pred[256,1280]{0,1:T(8,128)(4,1)} fusion(s32[256]{0:T(256)S(1)} %copy-done.30, s32[1280]{0:T(1024)S(1)} %constant_dynamic-update-slice_fusion.21, pred[1280]{0:T(1024)(128)(4,1)S(1)} %broadcast_compare_fusion, s32[1280]{0:T(1024)S(1)} %iota_add_fusion, s32[256]{0:T(256)S(1)} %iota_add_fusion.1), kind=kLoop, calls=%fused_computation.72 | loop fusion | flops 1638400 | bytes 341248 | tf_op jit(solution)/shard_map/and | solution.py:78
  36.9 1.6 collective-permute-done.2
  38.8 5.1 %collective-permute-done = bf16[256,256]{1,0:T(8,128)(2,1)S(1)} collective-permute-done((bf16[256,256]{1,0:T(8,128)(2,1)S(1)}, bf16[256,256]{1,0:T(8,128)(2,1)S(1)}, u32[]{:S(2)}, u32[]{:S(2)}) %collective-permute-start) | collective-permute-done | bytes 131104 | tf_op jit(solution)/shard_map/ppermute | solution.py:17
  43.9 5.9 %collective-permute-start.11 = (bf16[256,256]{1,0:T(8,128)(2,1)}, bf16[256,256]{1,0:T(8,128)(2,1)}, u32[]{:S(2)}, u32[]{:S(2)}) collective-permute-start(bf16[256,256]{1,0:T(8,128)(2,1)} %pad_maximum_fusion.8), channel_id=1, source_target_pairs={{0,2},{2,4},{4,6},{6,8},{8,10},{10,12},{12,14},{1,3},{3,5},{5,7},{... | collective-permute-start | bytes 393224 | tf_op jit(solution)/shard_map/ppermute | solution.py:17
  49.9 1.9 collective-permute-start.10
  51.8 5.3 %collective-permute-start.9 = (bf16[256,256]{1,0:T(8,128)(2,1)}, bf16[256,256]{1,0:T(8,128)(2,1)}, u32[]{:S(2)}, u32[]{:S(2)}) collective-permute-start(bf16[256,256]{1,0:T(8,128)(2,1)} %pad_maximum_fusion.8), channel_id=1, source_target_pairs={{0,6},{2,8},{4,10},{6,12},{8,14},{1,7},{3,9},{5,11},{7,13},{9,15},... | collective-permute-start | bytes 393224 | tf_op jit(solution)/shard_map/ppermute | solution.py:17
  57.1 1.9 collective-permute-start.8
  60.0 2.8 %fusion.117 = (f32[2,256]{1,0:T(2,128)S(1)}, f32[2,256,1280]{1,2,0:T(8,128)S(1)}) fusion(bf16[256,2,128]{0,2,1:T(8,128)(2,1)} %bitcast.265, s32[256,1280]{0,1:T(8,128)} %broadcast_subtract_fusion, s32[2]{0:T(128)} %get-tuple-element.61, pred[256,1280]{0,1:T(8,128)(4,1)} %compare_and_fusion, bf16[1280,256]{1,0:T(8,128)(2,1)} %copy-done.12), kind=kOutput, calls=%fused_computation.206 | convolution fusion | flops 171705600 | bytes 4721152 | tf_op jit(solution)/shard_map/sub | solution.py:33
  64.3 1.5 convolution_bitcast_fusion.10
  66.3 1.0 fusion.40
  68.8 1.7 copy.180
  70.5 5.4 %collective-permute-start.20 = (bf16[256,256]{0,1:T(8,128)(2,1)}, bf16[256,256]{0,1:T(8,128)(2,1)}, u32[]{:S(2)}, u32[]{:S(2)}) collective-permute-start(bf16[256,256]{0,1:T(8,128)(2,1)} %get-tuple-element.21), channel_id=1, source_target_pairs={{2,0},{4,2},{6,4},{8,6},{10,8},{12,10},{14,12},{3,1},{5,3},{7,5},{... | collective-permute-start | bytes 393224 | tf_op jit(solution)/shard_map/ppermute | solution.py:17
  76.0 1.3 collective-permute-start.23
  78.2 1.3 collective-permute-start.22
  80.4 1.9 collective-permute-start.21
  82.3 0.9 constant_dynamic-update-slice_fusion.8
  83.3 0.9 constant_dynamic-update-slice_fusion.7
  85.1 3.9 %fusion.116 = (f32[2,256]{1,0:T(2,128)S(1)}, f32[2,256,1280]{1,2,0:T(8,128)}) fusion(bf16[256,2,128]{0,2,1:T(8,128)(2,1)} %bitcast.263, s32[256,1280]{0,1:T(8,128)S(1)} %copy-done.3, s32[2]{0:T(128)S(1)} %get-tuple-element.62, pred[256,1280]{0,1:T(8,128)(4,1)} %compare_and_fusion, bf16[1280,256]{1,0:T(8,128)(2,1)S(1)} %constant_dynamic-update-slice_fusion.6), kind=kOutput, calls=%fused_computation.205 | convolution fusion | flops 171705600 | bytes 4721152 | tf_op jit(solution)/shard_map/sub | solution.py:33
  89.0 2.0 fusion.61
  95.3 3.0 %collective-permute-start.15 = (bf16[256,256]{1,0:T(8,128)(2,1)S(1)}, bf16[256,256]{1,0:T(8,128)(2,1)S(1)}, u32[]{:S(2)}, u32[]{:S(2)}) collective-permute-start(bf16[256,256]{1,0:T(8,128)(2,1)S(1)} %copy-done.19), channel_id=1, source_target_pairs={{0,2},{2,4},{4,6},{6,8},{8,10},{10,12},{12,14},{1,3},{3,5},{5,7},{... | collective-permute-start | bytes 393224 | tf_op jit(solution)/shard_map/ppermute | solution.py:17
  99.2 5.5 %collective-permute-start.14 = (bf16[256,256]{1,0:T(8,128)(2,1)S(1)}, bf16[256,256]{1,0:T(8,128)(2,1)}, u32[]{:S(2)}, u32[]{:S(2)}) collective-permute-start(bf16[256,256]{1,0:T(8,128)(2,1)S(1)} %copy-done.19), channel_id=1, source_target_pairs={{0,4},{2,6},{4,8},{6,10},{8,12},{10,14},{1,5},{3,7},{5,9},{7,11},{... | collective-permute-start | bytes 393224 | tf_op jit(solution)/shard_map/ppermute | solution.py:17
  104.8 4.1 %collective-permute-start.13 = (bf16[256,256]{1,0:T(8,128)(2,1)S(1)}, bf16[256,256]{1,0:T(8,128)(2,1)}, u32[]{:S(2)}, u32[]{:S(2)}) collective-permute-start(bf16[256,256]{1,0:T(8,128)(2,1)S(1)} %copy-done.19), channel_id=1, source_target_pairs={{0,6},{2,8},{4,10},{6,12},{8,14},{1,7},{3,9},{5,11},{7,13},{9,15},... | collective-permute-start | bytes 393224 | tf_op jit(solution)/shard_map/ppermute | solution.py:17
  108.9 1.9 collective-permute-start.12
  110.9 5.4 %collective-permute-start.24 = (bf16[256,256]{0,1:T(8,128)(2,1)}, bf16[256,256]{0,1:T(8,128)(2,1)}, u32[]{:S(2)}, u32[]{:S(2)}) collective-permute-start(bf16[256,256]{0,1:T(8,128)(2,1)} %get-tuple-element.25), channel_id=1, source_target_pairs={{2,0},{4,2},{6,4},{8,6},{10,8},{12,10},{14,12},{3,1},{5,3},{7,5},{... | collective-permute-start | bytes 393224 | tf_op jit(solution)/shard_map/ppermute | solution.py:17
  116.3 1.2 fusion.88
  118.9 1.3 collective-permute-start.27
  121.1 1.3 collective-permute-start.26
  123.3 2.1 %collective-permute-start.25 = (bf16[256,256]{0,1:T(8,128)(2,1)}, bf16[256,256]{0,1:T(8,128)(2,1)}, u32[]{:S(2)}, u32[]{:S(2)}) collective-permute-start(bf16[256,256]{0,1:T(8,128)(2,1)} %get-tuple-element.28), channel_id=1, source_target_pairs={{4,0},{6,2},{8,4},{10,6},{12,8},{14,10},{5,1},{7,3},{9,5},{11,7},{... | collective-permute-start | bytes 393224 | tf_op jit(solution)/shard_map/ppermute | solution.py:17
  126.4 4.0 %fusion.115 = (f32[2,256]{1,0:T(2,128)S(1)}, f32[2,256,1280]{1,2,0:T(8,128)}) fusion(bf16[256,2,128]{0,2,1:T(8,128)(2,1)S(1)} %bitcast.261, s32[256,1280]{0,1:T(8,128)} %broadcast_subtract_fusion, s32[2]{0:T(128)S(1)} %get-tuple-element.64, pred[256,1280]{0,1:T(8,128)(4,1)S(1)} %copy-done.23, bf16[1280,256]{1,0:T(8,128)(2,1)S(1)} %constant_dynamic-update-slice_fusion.11), kind=kOutput, calls=%fused_computation.204 | convolution fusion | flops 171705600 | bytes 4721152 | tf_op jit(solution)/shard_map/sub | solution.py:33
  130.4 2.0 fusion.62
  134.6 1.0 fusion.42
  136.2 3.7 %collective-permute-start.19 = (bf16[256,256]{1,0:T(8,128)(2,1)}, bf16[256,256]{1,0:T(8,128)(2,1)}, u32[]{:S(2)}, u32[]{:S(2)}) collective-permute-start(bf16[256,256]{1,0:T(8,128)(2,1)} %pad_maximum_fusion.10), channel_id=1, source_target_pairs={{0,2},{2,4},{4,6},{6,8},{8,10},{10,12},{12,14},{1,3},{3,5},{5,7},{... | collective-permute-start | bytes 393224 | tf_op jit(solution)/shard_map/ppermute | solution.py:17
  140.8 4.2 %collective-permute-start.18 = (bf16[256,256]{1,0:T(8,128)(2,1)}, bf16[256,256]{1,0:T(8,128)(2,1)}, u32[]{:S(2)}, u32[]{:S(2)}) collective-permute-start(bf16[256,256]{1,0:T(8,128)(2,1)} %pad_maximum_fusion.10), channel_id=1, source_target_pairs={{0,4},{2,6},{4,8},{6,10},{8,12},{10,14},{1,5},{3,7},{5,9},{7,11},{... | collective-permute-start | bytes 393224 | tf_op jit(solution)/shard_map/ppermute | solution.py:17
  145.1 4.5 %collective-permute-start.17 = (bf16[256,256]{1,0:T(8,128)(2,1)}, bf16[256,256]{1,0:T(8,128)(2,1)}, u32[]{:S(2)}, u32[]{:S(2)}) collective-permute-start(bf16[256,256]{1,0:T(8,128)(2,1)} %pad_maximum_fusion.10), channel_id=1, source_target_pairs={{0,6},{2,8},{4,10},{6,12},{8,14},{1,7},{3,9},{5,11},{7,13},{9,15},... | collective-permute-start | bytes 393224 | tf_op jit(solution)/shard_map/ppermute | solution.py:17
  149.5 1.9 collective-permute-start.16
  151.5 4.8 %collective-permute-start.28 = (bf16[256,256]{0,1:T(8,128)(2,1)}, bf16[256,256]{0,1:T(8,128)(2,1)}, u32[]{:S(2)}, u32[]{:S(2)}) collective-permute-start(bf16[256,256]{0,1:T(8,128)(2,1)} %get-tuple-element.29), channel_id=1, source_target_pairs={{2,0},{4,2},{6,4},{8,6},{10,8},{12,10},{14,12},{3,1},{5,3},{7,5},{... | collective-permute-start | bytes 393224 | tf_op jit(solution)/shard_map/ppermute | solution.py:17
  156.3 1.0 fusion.82
  158.1 1.7 copy.182
  159.7 1.3 collective-permute-start.31
  161.9 1.3 collective-permute-start.30
  164.2 1.9 collective-permute-start.29
  167.9 0.9 constant_dynamic-update-slice_fusion.16
  168.9 3.8 %fusion.114 = (f32[2,256]{1,0:T(2,128)S(1)}, f32[2,256,1280]{1,2,0:T(8,128)}) fusion(bf16[256,2,128]{0,2,1:T(8,128)(2,1)S(1)} %bitcast.259, s32[256,1280]{0,1:T(8,128)S(1)} %copy-done.4, s32[2]{0:T(128)S(1)} %get-tuple-element.63, pred[256,1280]{0,1:T(8,128)(4,1)} %compare_and_fusion, bf16[1280,256]{1,0:T(8,128)(2,1)S(1)} %constant_dynamic-update-slice_fusion.16), kind=kOutput, calls=%fused_computation.203 | convolution fusion | flops 171705600 | bytes 4721152 | tf_op jit(solution)/shard_map/sub | solution.py:33
  172.7 2.0 fusion.63
  178.9 2.0 %collective-permute-start.32 = (bf16[256,256]{0,1:T(8,128)(2,1)}, bf16[256,256]{0,1:T(8,128)(2,1)}, u32[]{:S(2)}, u32[]{:S(2)}) collective-permute-start(bf16[256,256]{0,1:T(8,128)(2,1)} %get-tuple-element.33), channel_id=1, source_target_pairs={{2,0},{4,2},{6,4},{8,6},{10,8},{12,10},{14,12},{3,1},{5,3},{7,5},{... | collective-permute-start | bytes 393224 | tf_op jit(solution)/shard_map/ppermute | solution.py:17
  180.9 1.3 collective-permute-start.35
  182.3 1.3 collective-permute-start.34
  183.6 1.9 collective-permute-start.33
  185.5 1.2 fusion.76
  187.7 4.6 %collective-permute-done.35 = bf16[256,256]{0,1:T(8,128)(2,1)} collective-permute-done((bf16[256,256]{0,1:T(8,128)(2,1)S(1)}, bf16[256,256]{0,1:T(8,128)(2,1)}, u32[]{:S(2)}, u32[]{:S(2)}) %collective-permute-start.35) | collective-permute-done | bytes 131104 | tf_op jit(solution)/shard_map/ppermute | solution.py:17
  192.4 1.0 collective-permute-done.34
  193.4 4.9 %collective-permute-done.33 = bf16[256,256]{0,1:T(8,128)(2,1)} collective-permute-done((bf16[256,256]{0,1:T(8,128)(2,1)S(1)}, bf16[256,256]{0,1:T(8,128)(2,1)}, u32[]{:S(2)}, u32[]{:S(2)}) %collective-permute-start.33) | collective-permute-done | bytes 131104 | tf_op jit(solution)/shard_map/ppermute | solution.py:17
  198.3 1.2 fusion.70
  (181 shorter events, 40.1 us)
Async XLA Ops:
  0.6 16.9 %copy-start.25 = (bf16[256,512]{1,0:T(8,128)(2,1)S(1)}, bf16[256,512]{1,0:T(8,128)(2,1)}, u32[]{:S(2)}) copy-start(bf16[256,512]{1,0:T(8,128)(2,1)} %param.9) | copy-start | bytes 786436
  0.6 16.9 %copy-start.24 = (bf16[256,512]{1,0:T(8,128)(2,1)S(1)}, bf16[256,512]{1,0:T(8,128)(2,1)}, u32[]{:S(2)}) copy-start(bf16[256,512]{1,0:T(8,128)(2,1)} %param.8) | copy-start | bytes 786436
  0.7 34.2 %collective-permute-start.7 = (s32[256]{0:T(256)}, s32[256]{0:T(256)S(1)}, u32[]{:S(2)}, u32[]{:S(2)}) collective-permute-start(s32[256]{0:T(256)} %param.11), channel_id=1, source_target_pairs={{0,2},{2,4},{4,6},{6,8},{8,10},{10,12},{12,14},{1,3},{3,5},{5,7},{... | collective-permute-start | bytes 3080 | tf_op jit(solution)/shard_map/ppermute | solution.py:17
  4.2 29.3 %collective-permute-start.6 = (s32[256]{0:T(256)}, s32[256]{0:T(256)S(1)}, u32[]{:S(2)}, u32[]{:S(2)}) collective-permute-start(s32[256]{0:T(256)} %param.11), channel_id=1, source_target_pairs={{0,4},{2,6},{4,8},{6,10},{8,12},{10,14},{1,5},{3,7},{5,9},{7,11},{... | collective-permute-start | bytes 3080 | tf_op jit(solution)/shard_map/ppermute | solution.py:17
  7.7 24.5 %collective-permute-start.5 = (s32[256]{0:T(256)}, s32[256]{0:T(256)S(1)}, u32[]{:S(2)}, u32[]{:S(2)}) collective-permute-start(s32[256]{0:T(256)} %param.11), channel_id=1, source_target_pairs={{0,6},{2,8},{4,10},{6,12},{8,14},{1,7},{3,9},{5,11},{7,13},{9,15},... | collective-permute-start | bytes 3080 | tf_op jit(solution)/shard_map/ppermute | solution.py:17
  10.6 19.6 %collective-permute-start.4 = (s32[256]{0:T(256)}, s32[256]{0:T(256)S(1)}, u32[]{:S(2)}, u32[]{:S(2)}) collective-permute-start(s32[256]{0:T(256)} %param.11), channel_id=1, source_target_pairs={{0,8},{2,10},{4,12},{6,14},{1,9},{3,11},{5,13},{7,15},{16,24},{18,... | collective-permute-start | bytes 3080 | tf_op jit(solution)/shard_map/ppermute | solution.py:17
  13.9 6.6 %copy-start.30 = (s32[256]{0:T(256)S(1)}, s32[256]{0:T(256)}, u32[]{:S(2)}) copy-start(s32[256]{0:T(256)} %param.11) | copy-start | bytes 3076
  13.9 6.6 %copy-start.32 = (f32[4]{0:T(128)S(1)}, f32[4]{0:T(128)}, u32[]{:S(2)}) copy-start(f32[4]{0:T(128)} %param.12) | copy-start | bytes 52
  13.9 6.7 %copy-start.31 = (s32[8]{0:T(128)S(1)}, s32[8]{0:T(128)}, u32[]{:S(2)}) copy-start(s32[8]{0:T(128)} %param.13) | copy-start | bytes 100
  13.9 7.3 %all-to-all-start = ((bf16[128,2,1024]{0,2,1:T(8,128)(2,1)}), bf16[128,2,1024]{0,2,1:T(8,128)(2,1)S(1)}, u32[]{:S(2)}, u32[]{:S(2)}) async-start(bf16[128,2,1024]{0,2,1:T(8,128)(2,1)} %bitcast.5), calls=%async_computation | async-start | bytes 1048576 | tf_op jit(solution)/shard_map/all_to_all | solution.py:69
  17.7 19.2 %collective-permute-start.3 = (bf16[256,256]{1,0:T(8,128)(2,1)S(1)}, bf16[256,256]{1,0:T(8,128)(2,1)S(1)}, u32[]{:S(2)}, u32[]{:S(2)}) collective-permute-start(bf16[256,256]{1,0:T(8,128)(2,1)S(1)} %pad_maximum_fusion.7), channel_id=1, source_target_pairs={{0,2},{2,4},{4,6},{6,8},{8,10},{10,12},{12,14},{1,3},{3,5},{5,7},{... | collective-permute-start | bytes 393224 | tf_op jit(solution)/shard_map/ppermute | solution.py:17
  26.2 36.8 %copy-start.6 = (bf16[256,256]{0,1:T(8,128)(2,1)}, bf16[256,256]{0,1:T(8,128)(2,1)S(1)}, u32[]{:S(2)}) copy-start(bf16[256,256]{0,1:T(8,128)(2,1)S(1)} %copy.150) | copy-start | bytes 393220
  30.2 8.3 %collective-permute-start.2 = (bf16[256,256]{1,0:T(8,128)(2,1)S(1)}, bf16[256,256]{1,0:T(8,128)(2,1)S(1)}, u32[]{:S(2)}, u32[]{:S(2)}) collective-permute-start(bf16[256,256]{1,0:T(8,128)(2,1)S(1)} %pad_maximum_fusion.7), channel_id=1, source_target_pairs={{0,4},{2,6},{4,8},{6,10},{8,12},{10,14},{1,5},{3,7},{5,9},{7,11},{... | collective-permute-start | bytes 393224 | tf_op jit(solution)/shard_map/ppermute | solution.py:17
  32.2 6.7 %collective-permute-start.1 = (bf16[256,256]{1,0:T(8,128)(2,1)S(1)}, bf16[256,256]{1,0:T(8,128)(2,1)S(1)}, u32[]{:S(2)}, u32[]{:S(2)}) collective-permute-start(bf16[256,256]{1,0:T(8,128)(2,1)S(1)} %pad_maximum_fusion.7), channel_id=1, source_target_pairs={{0,6},{2,8},{4,10},{6,12},{8,14},{1,7},{3,9},{5,11},{7,13},{9,15},... | collective-permute-start | bytes 393224 | tf_op jit(solution)/shard_map/ppermute | solution.py:17
  33.5 10.4 %collective-permute-start = (bf16[256,256]{1,0:T(8,128)(2,1)S(1)}, bf16[256,256]{1,0:T(8,128)(2,1)S(1)}, u32[]{:S(2)}, u32[]{:S(2)}) collective-permute-start(bf16[256,256]{1,0:T(8,128)(2,1)S(1)} %pad_maximum_fusion.7), channel_id=1, source_target_pairs={{0,8},{2,10},{4,12},{6,14},{1,9},{3,11},{5,13},{7,15},{16,24},{18,... | collective-permute-start | bytes 393224 | tf_op jit(solution)/shard_map/ppermute | solution.py:17
  43.9 39.3 %collective-permute-start.11 = (bf16[256,256]{1,0:T(8,128)(2,1)}, bf16[256,256]{1,0:T(8,128)(2,1)}, u32[]{:S(2)}, u32[]{:S(2)}) collective-permute-start(bf16[256,256]{1,0:T(8,128)(2,1)} %pad_maximum_fusion.8), channel_id=1, source_target_pairs={{0,2},{2,4},{4,6},{6,8},{8,10},{10,12},{12,14},{1,3},{3,5},{5,7},{... | collective-permute-start | bytes 393224 | tf_op jit(solution)/shard_map/ppermute | solution.py:17
  49.9 30.5 %collective-permute-start.10 = (bf16[256,256]{1,0:T(8,128)(2,1)}, bf16[256,256]{1,0:T(8,128)(2,1)}, u32[]{:S(2)}, u32[]{:S(2)}) collective-permute-start(bf16[256,256]{1,0:T(8,128)(2,1)} %pad_maximum_fusion.8), channel_id=1, source_target_pairs={{0,4},{2,6},{4,8},{6,10},{8,12},{10,14},{1,5},{3,7},{5,9},{7,11},{... | collective-permute-start | bytes 393224 | tf_op jit(solution)/shard_map/ppermute | solution.py:17
  51.8 26.4 %collective-permute-start.9 = (bf16[256,256]{1,0:T(8,128)(2,1)}, bf16[256,256]{1,0:T(8,128)(2,1)}, u32[]{:S(2)}, u32[]{:S(2)}) collective-permute-start(bf16[256,256]{1,0:T(8,128)(2,1)} %pad_maximum_fusion.8), channel_id=1, source_target_pairs={{0,6},{2,8},{4,10},{6,12},{8,14},{1,7},{3,9},{5,11},{7,13},{9,15},... | collective-permute-start | bytes 393224 | tf_op jit(solution)/shard_map/ppermute | solution.py:17
  57.1 18.8 %collective-permute-start.8 = (bf16[256,256]{1,0:T(8,128)(2,1)}, bf16[256,256]{1,0:T(8,128)(2,1)}, u32[]{:S(2)}, u32[]{:S(2)}) collective-permute-start(bf16[256,256]{1,0:T(8,128)(2,1)} %pad_maximum_fusion.8), channel_id=1, source_target_pairs={{0,8},{2,10},{4,12},{6,14},{1,9},{3,11},{5,13},{7,15},{16,24},{18,... | collective-permute-start | bytes 393224 | tf_op jit(solution)/shard_map/ppermute | solution.py:17
  64.2 1.5 copy-start.7
  68.0 17.1 %copy-start.3 = (s32[256,1280]{0,1:T(8,128)S(1)}, s32[256,1280]{0,1:T(8,128)}, u32[]{:S(2)}) copy-start(s32[256,1280]{0,1:T(8,128)} %broadcast_subtract_fusion) | copy-start | bytes 3932164
  70.5 28.7 %collective-permute-start.20 = (bf16[256,256]{0,1:T(8,128)(2,1)}, bf16[256,256]{0,1:T(8,128)(2,1)}, u32[]{:S(2)}, u32[]{:S(2)}) collective-permute-start(bf16[256,256]{0,1:T(8,128)(2,1)} %get-tuple-element.21), channel_id=1, source_target_pairs={{2,0},{4,2},{6,4},{8,6},{10,8},{12,10},{14,12},{3,1},{5,3},{7,5},{... | collective-permute-start | bytes 393224 | tf_op jit(solution)/shard_map/ppermute | solution.py:17
  76.0 28.8 %collective-permute-start.23 = (bf16[256,256]{0,1:T(8,128)(2,1)}, bf16[256,256]{0,1:T(8,128)(2,1)}, u32[]{:S(2)}, u32[]{:S(2)}) collective-permute-start(bf16[256,256]{0,1:T(8,128)(2,1)} %get-tuple-element.22), channel_id=1, source_target_pairs={{8,0},{10,2},{12,4},{14,6},{9,1},{11,3},{13,5},{15,7},{24,16},{26,... | collective-permute-start | bytes 393224 | tf_op jit(solution)/shard_map/ppermute | solution.py:17
  78.2 30.8 %collective-permute-start.22 = (bf16[256,256]{0,1:T(8,128)(2,1)}, bf16[256,256]{0,1:T(8,128)(2,1)}, u32[]{:S(2)}, u32[]{:S(2)}) collective-permute-start(bf16[256,256]{0,1:T(8,128)(2,1)} %get-tuple-element.23), channel_id=1, source_target_pairs={{6,0},{8,2},{10,4},{12,6},{14,8},{7,1},{9,3},{11,5},{13,7},{15,9},... | collective-permute-start | bytes 393224 | tf_op jit(solution)/shard_map/ppermute | solution.py:17
  80.4 30.5 %collective-permute-start.21 = (bf16[256,256]{0,1:T(8,128)(2,1)}, bf16[256,256]{0,1:T(8,128)(2,1)}, u32[]{:S(2)}, u32[]{:S(2)}) collective-permute-start(bf16[256,256]{0,1:T(8,128)(2,1)} %get-tuple-element.24), channel_id=1, source_target_pairs={{4,0},{6,2},{8,4},{10,6},{12,8},{14,10},{5,1},{7,3},{9,5},{11,7},{... | collective-permute-start | bytes 393224 | tf_op jit(solution)/shard_map/ppermute | solution.py:17
  85.1 5.9 %copy-start.8 = (bf16[1280,256]{1,0:T(8,128)(2,1)}, bf16[1280,256]{1,0:T(8,128)(2,1)S(1)}, u32[]{:S(2)}) copy-start(bf16[1280,256]{1,0:T(8,128)(2,1)S(1)} %constant_dynamic-update-slice_fusion.6) | copy-start | bytes 1966084
  89.0 2.0 copy-start.5
  91.1 1.7 copy-start.1
  91.5 1.6 copy-start.9
  95.3 31.0 %collective-permute-start.15 = (bf16[256,256]{1,0:T(8,128)(2,1)S(1)}, bf16[256,256]{1,0:T(8,128)(2,1)S(1)}, u32[]{:S(2)}, u32[]{:S(2)}) collective-permute-start(bf16[256,256]{1,0:T(8,128)(2,1)S(1)} %copy-done.19), channel_id=1, source_target_pairs={{0,2},{2,4},{4,6},{6,8},{8,10},{10,12},{12,14},{1,3},{3,5},{5,7},{... | collective-permute-start | bytes 393224 | tf_op jit(solution)/shard_map/ppermute | solution.py:17
  99.2 24.1 %collective-permute-start.14 = (bf16[256,256]{1,0:T(8,128)(2,1)S(1)}, bf16[256,256]{1,0:T(8,128)(2,1)}, u32[]{:S(2)}, u32[]{:S(2)}) collective-permute-start(bf16[256,256]{1,0:T(8,128)(2,1)S(1)} %copy-done.19), channel_id=1, source_target_pairs={{0,4},{2,6},{4,8},{6,10},{8,12},{10,14},{1,5},{3,7},{5,9},{7,11},{... | collective-permute-start | bytes 393224 | tf_op jit(solution)/shard_map/ppermute | solution.py:17
  104.8 16.3 %collective-permute-start.13 = (bf16[256,256]{1,0:T(8,128)(2,1)S(1)}, bf16[256,256]{1,0:T(8,128)(2,1)}, u32[]{:S(2)}, u32[]{:S(2)}) collective-permute-start(bf16[256,256]{1,0:T(8,128)(2,1)S(1)} %copy-done.19), channel_id=1, source_target_pairs={{0,6},{2,8},{4,10},{6,12},{8,14},{1,7},{3,9},{5,11},{7,13},{9,15},... | collective-permute-start | bytes 393224 | tf_op jit(solution)/shard_map/ppermute | solution.py:17
  108.9 9.9 %collective-permute-start.12 = (bf16[256,256]{1,0:T(8,128)(2,1)S(1)}, bf16[256,256]{1,0:T(8,128)(2,1)}, u32[]{:S(2)}, u32[]{:S(2)}) collective-permute-start(bf16[256,256]{1,0:T(8,128)(2,1)S(1)} %copy-done.19), channel_id=1, source_target_pairs={{0,8},{2,10},{4,12},{6,14},{1,9},{3,11},{5,13},{7,15},{16,24},{18,... | collective-permute-start | bytes 393224 | tf_op jit(solution)/shard_map/ppermute | solution.py:17
  110.9 29.9 %collective-permute-start.24 = (bf16[256,256]{0,1:T(8,128)(2,1)}, bf16[256,256]{0,1:T(8,128)(2,1)}, u32[]{:S(2)}, u32[]{:S(2)}) collective-permute-start(bf16[256,256]{0,1:T(8,128)(2,1)} %get-tuple-element.25), channel_id=1, source_target_pairs={{2,0},{4,2},{6,4},{8,6},{10,8},{12,10},{14,12},{3,1},{5,3},{7,5},{... | collective-permute-start | bytes 393224 | tf_op jit(solution)/shard_map/ppermute | solution.py:17
  117.4 9.0 %copy-start.15 = (bf16[256,256]{0,1:T(8,128)(2,1)S(1)}, bf16[256,256]{0,1:T(8,128)(2,1)}, u32[]{:S(2)}) copy-start(bf16[256,256]{0,1:T(8,128)(2,1)} %copy.236) | copy-start | bytes 393220
  117.4 9.0 %copy-start.23 = (pred[256,1280]{0,1:T(8,128)(4,1)S(1)}, pred[256,1280]{0,1:T(8,128)(4,1)}, u32[]{:S(2)}) copy-start(pred[256,1280]{0,1:T(8,128)(4,1)} %compare_and_fusion) | copy-start | bytes 983044
  118.9 26.2 %collective-permute-start.27 = (bf16[256,256]{0,1:T(8,128)(2,1)}, bf16[256,256]{0,1:T(8,128)(2,1)S(1)}, u32[]{:S(2)}, u32[]{:S(2)}) collective-permute-start(bf16[256,256]{0,1:T(8,128)(2,1)} %get-tuple-element.26), channel_id=1, source_target_pairs={{8,0},{10,2},{12,4},{14,6},{9,1},{11,3},{13,5},{15,7},{24,16},{26,... | collective-permute-start | bytes 393224 | tf_op jit(solution)/shard_map/ppermute | solution.py:17
  121.1 28.4 %collective-permute-start.26 = (bf16[256,256]{0,1:T(8,128)(2,1)}, bf16[256,256]{0,1:T(8,128)(2,1)S(1)}, u32[]{:S(2)}, u32[]{:S(2)}) collective-permute-start(bf16[256,256]{0,1:T(8,128)(2,1)} %get-tuple-element.27), channel_id=1, source_target_pairs={{6,0},{8,2},{10,4},{12,6},{14,8},{7,1},{9,3},{11,5},{13,7},{15,9},... | collective-permute-start | bytes 393224 | tf_op jit(solution)/shard_map/ppermute | solution.py:17
  123.3 28.2 %collective-permute-start.25 = (bf16[256,256]{0,1:T(8,128)(2,1)}, bf16[256,256]{0,1:T(8,128)(2,1)}, u32[]{:S(2)}, u32[]{:S(2)}) collective-permute-start(bf16[256,256]{0,1:T(8,128)(2,1)} %get-tuple-element.28), channel_id=1, source_target_pairs={{4,0},{6,2},{8,4},{10,6},{12,8},{14,10},{5,1},{7,3},{9,5},{11,7},{... | collective-permute-start | bytes 393224 | tf_op jit(solution)/shard_map/ppermute | solution.py:17
  132.3 1.7 copy-start.2
  136.2 30.8 %collective-permute-start.19 = (bf16[256,256]{1,0:T(8,128)(2,1)}, bf16[256,256]{1,0:T(8,128)(2,1)}, u32[]{:S(2)}, u32[]{:S(2)}) collective-permute-start(bf16[256,256]{1,0:T(8,128)(2,1)} %pad_maximum_fusion.10), channel_id=1, source_target_pairs={{0,2},{2,4},{4,6},{6,8},{8,10},{10,12},{12,14},{1,3},{3,5},{5,7},{... | collective-permute-start | bytes 393224 | tf_op jit(solution)/shard_map/ppermute | solution.py:17
  140.8 23.3 %collective-permute-start.18 = (bf16[256,256]{1,0:T(8,128)(2,1)}, bf16[256,256]{1,0:T(8,128)(2,1)}, u32[]{:S(2)}, u32[]{:S(2)}) collective-permute-start(bf16[256,256]{1,0:T(8,128)(2,1)} %pad_maximum_fusion.10), channel_id=1, source_target_pairs={{0,4},{2,6},{4,8},{6,10},{8,12},{10,14},{1,5},{3,7},{5,9},{7,11},{... | collective-permute-start | bytes 393224 | tf_op jit(solution)/shard_map/ppermute | solution.py:17
  145.1 16.9 %collective-permute-start.17 = (bf16[256,256]{1,0:T(8,128)(2,1)}, bf16[256,256]{1,0:T(8,128)(2,1)}, u32[]{:S(2)}, u32[]{:S(2)}) collective-permute-start(bf16[256,256]{1,0:T(8,128)(2,1)} %pad_maximum_fusion.10), channel_id=1, source_target_pairs={{0,6},{2,8},{4,10},{6,12},{8,14},{1,7},{3,9},{5,11},{7,13},{9,15},... | collective-permute-start | bytes 393224 | tf_op jit(solution)/shard_map/ppermute | solution.py:17
  149.5 10.2 %collective-permute-start.16 = (bf16[256,256]{1,0:T(8,128)(2,1)}, bf16[256,256]{1,0:T(8,128)(2,1)}, u32[]{:S(2)}, u32[]{:S(2)}) collective-permute-start(bf16[256,256]{1,0:T(8,128)(2,1)} %pad_maximum_fusion.10), channel_id=1, source_target_pairs={{0,8},{2,10},{4,12},{6,14},{1,9},{3,11},{5,13},{7,15},{16,24},{18,... | collective-permute-start | bytes 393224 | tf_op jit(solution)/shard_map/ppermute | solution.py:17
  151.5 29.5 %collective-permute-start.28 = (bf16[256,256]{0,1:T(8,128)(2,1)}, bf16[256,256]{0,1:T(8,128)(2,1)}, u32[]{:S(2)}, u32[]{:S(2)}) collective-permute-start(bf16[256,256]{0,1:T(8,128)(2,1)} %get-tuple-element.29), channel_id=1, source_target_pairs={{2,0},{4,2},{6,4},{8,6},{10,8},{12,10},{14,12},{3,1},{5,3},{7,5},{... | collective-permute-start | bytes 393224 | tf_op jit(solution)/shard_map/ppermute | solution.py:17
  157.4 11.5 %copy-start.4 = (s32[256,1280]{0,1:T(8,128)S(1)}, s32[256,1280]{0,1:T(8,128)}, u32[]{:S(2)}) copy-start(s32[256,1280]{0,1:T(8,128)} %broadcast_subtract_fusion) | copy-start | bytes 3932164
  157.4 11.5 %copy-start.14 = (bf16[256,256]{0,1:T(8,128)(2,1)S(1)}, bf16[256,256]{0,1:T(8,128)(2,1)}, u32[]{:S(2)}) copy-start(bf16[256,256]{0,1:T(8,128)(2,1)} %copy.237) | copy-start | bytes 393220
  159.7 22.5 %collective-permute-start.31 = (bf16[256,256]{0,1:T(8,128)(2,1)}, bf16[256,256]{0,1:T(8,128)(2,1)}, u32[]{:S(2)}, u32[]{:S(2)}) collective-permute-start(bf16[256,256]{0,1:T(8,128)(2,1)} %get-tuple-element.30), channel_id=1, source_target_pairs={{8,0},{10,2},{12,4},{14,6},{9,1},{11,3},{13,5},{15,7},{24,16},{26,... | collective-permute-start | bytes 393224 | tf_op jit(solution)/shard_map/ppermute | solution.py:17
  161.9 21.6 %collective-permute-start.30 = (bf16[256,256]{0,1:T(8,128)(2,1)}, bf16[256,256]{0,1:T(8,128)(2,1)}, u32[]{:S(2)}, u32[]{:S(2)}) collective-permute-start(bf16[256,256]{0,1:T(8,128)(2,1)} %get-tuple-element.31), channel_id=1, source_target_pairs={{6,0},{8,2},{10,4},{12,6},{14,8},{7,1},{9,3},{11,5},{13,7},{15,9},... | collective-permute-start | bytes 393224 | tf_op jit(solution)/shard_map/ppermute | solution.py:17
  164.2 21.3 %collective-permute-start.29 = (bf16[256,256]{0,1:T(8,128)(2,1)}, bf16[256,256]{0,1:T(8,128)(2,1)}, u32[]{:S(2)}, u32[]{:S(2)}) collective-permute-start(bf16[256,256]{0,1:T(8,128)(2,1)} %get-tuple-element.32), channel_id=1, source_target_pairs={{4,0},{6,2},{8,4},{10,6},{12,8},{14,10},{5,1},{7,3},{9,5},{11,7},{... | collective-permute-start | bytes 393224 | tf_op jit(solution)/shard_map/ppermute | solution.py:17
  168.9 5.8 %copy-start.10 = (bf16[1280,256]{1,0:T(8,128)(2,1)}, bf16[1280,256]{1,0:T(8,128)(2,1)S(1)}, u32[]{:S(2)}) copy-start(bf16[1280,256]{1,0:T(8,128)(2,1)S(1)} %constant_dynamic-update-slice_fusion.16) | copy-start | bytes 1966084
  174.7 1.7 copy-start
  175.1 1.6 copy-start.11
  178.9 7.9 %copy-start.20 = (bf16[256,256]{1,0:T(8,128)(2,1)S(1)}, bf16[256,256]{1,0:T(8,128)(2,1)}, u32[]{:S(2)}) copy-start(bf16[256,256]{1,0:T(8,128)(2,1)} %copy.180) | copy-start | bytes 393220
  178.9 7.9 %copy-start.21 = (bf16[256,256]{1,0:T(8,128)(2,1)S(1)}, bf16[256,256]{1,0:T(8,128)(2,1)}, u32[]{:S(2)}) copy-start(bf16[256,256]{1,0:T(8,128)(2,1)} %copy.181) | copy-start | bytes 393220
  178.9 7.9 %copy-start.22 = (bf16[256,256]{1,0:T(8,128)(2,1)S(1)}, bf16[256,256]{1,0:T(8,128)(2,1)}, u32[]{:S(2)}) copy-start(bf16[256,256]{1,0:T(8,128)(2,1)} %copy.182) | copy-start | bytes 393220
  178.9 8.8 %collective-permute-start.32 = (bf16[256,256]{0,1:T(8,128)(2,1)}, bf16[256,256]{0,1:T(8,128)(2,1)}, u32[]{:S(2)}, u32[]{:S(2)}) collective-permute-start(bf16[256,256]{0,1:T(8,128)(2,1)} %get-tuple-element.33), channel_id=1, source_target_pairs={{2,0},{4,2},{6,4},{8,6},{10,8},{12,10},{14,12},{3,1},{5,3},{7,5},{... | collective-permute-start | bytes 393224 | tf_op jit(solution)/shard_map/ppermute | solution.py:17
  180.9 11.4 %collective-permute-start.35 = (bf16[256,256]{0,1:T(8,128)(2,1)S(1)}, bf16[256,256]{0,1:T(8,128)(2,1)}, u32[]{:S(2)}, u32[]{:S(2)}) collective-permute-start(bf16[256,256]{0,1:T(8,128)(2,1)S(1)} %get-tuple-element.34), channel_id=1, source_target_pairs={{8,0},{10,2},{12,4},{14,6},{9,1},{11,3},{13,5},{15,7},{24,16},{26,... | collective-permute-start | bytes 393224 | tf_op jit(solution)/shard_map/ppermute | solution.py:17
  182.3 11.1 %collective-permute-start.34 = (bf16[256,256]{0,1:T(8,128)(2,1)S(1)}, bf16[256,256]{0,1:T(8,128)(2,1)}, u32[]{:S(2)}, u32[]{:S(2)}) collective-permute-start(bf16[256,256]{0,1:T(8,128)(2,1)S(1)} %get-tuple-element.35), channel_id=1, source_target_pairs={{6,0},{8,2},{10,4},{12,6},{14,8},{7,1},{9,3},{11,5},{13,7},{15,9},... | collective-permute-start | bytes 393224 | tf_op jit(solution)/shard_map/ppermute | solution.py:17
  183.6 14.7 %collective-permute-start.33 = (bf16[256,256]{0,1:T(8,128)(2,1)S(1)}, bf16[256,256]{0,1:T(8,128)(2,1)}, u32[]{:S(2)}, u32[]{:S(2)}) collective-permute-start(bf16[256,256]{0,1:T(8,128)(2,1)S(1)} %get-tuple-element.36), channel_id=1, source_target_pairs={{4,0},{6,2},{8,4},{10,6},{12,8},{14,10},{5,1},{7,3},{9,5},{11,7},{... | collective-permute-start | bytes 393224 | tf_op jit(solution)/shard_map/ppermute | solution.py:17
  187.7 11.8 %copy-start.27 = (bf16[256,128]{0,1:T(8,128)(2,1)S(1)}, bf16[256,128]{0,1:T(8,128)(2,1)}, u32[]{:S(2)}) copy-start(bf16[256,128]{0,1:T(8,128)(2,1)} %get-tuple-element.53) | copy-start | bytes 196612
  187.7 11.8 %copy-start.29 = (bf16[256,128]{0,1:T(8,128)(2,1)S(1)}, bf16[256,128]{0,1:T(8,128)(2,1)}, u32[]{:S(2)}) copy-start(bf16[256,128]{0,1:T(8,128)(2,1)} %get-tuple-element.55) | copy-start | bytes 196612
  187.7 12.7 %copy-start.26 = (bf16[256,128]{0,1:T(8,128)(2,1)S(1)}, bf16[256,128]{0,1:T(8,128)(2,1)}, u32[]{:S(2)}) copy-start(bf16[256,128]{0,1:T(8,128)(2,1)} %get-tuple-element.54) | copy-start | bytes 196612
  187.7 12.7 %copy-start.28 = (bf16[256,128]{0,1:T(8,128)(2,1)S(1)}, bf16[256,128]{0,1:T(8,128)(2,1)}, u32[]{:S(2)}) copy-start(bf16[256,128]{0,1:T(8,128)(2,1)} %get-tuple-element.56) | copy-start | bytes 196612
  (6 other events, 5.8 us)

commit v2 on v1

v2 whole, which is shorter than its diff:
```python
import functools
import jax
import jax.numpy as jnp
from jax import lax
from jax.experimental import pallas as pl
from jax.experimental.pallas import tpu as pltpu
from jax.sharding import PartitionSpec as P

HEAD_DIMENSION = 128
WINDOW = 1024
KV_PER_CHUNK = 4
score_scale = 168.0 ** (-0.5)


def _nt(a, b):
    return lax.dot_general(a, b, (((1,), (1,)), ((), ())), preferred_element_type=jnp.float32)


def _tn(a, b):
    return lax.dot_general(a, b, (((0,), (0,)), ((), ())), preferred_element_type=jnp.float32)


def _nn(a, b):
    return lax.dot_general(a, b, (((1,), (0,)), ((), ())), preferred_element_type=jnp.float32)


def attention_kernel(win_ref, qid_ref, kid_ref, q_ref, g_ref, *rest, pieces, group_size):
    kv_refs = rest[:pieces]
    dq_ref = rest[pieces]
    own_ref = rest[pieces + 1]
    cross_refs = rest[pieces + 2 :]
    d = HEAD_DIMENSION
    rows = q_ref.shape[0]
    piece_rows = kv_refs[0].shape[0]
    width = kv_refs[0].shape[1] // 2
    key_count = pieces * piece_rows
    row = lax.broadcasted_iota(jnp.int32, (rows, key_count), 0)
    col = lax.broadcasted_iota(jnp.int32, (rows, key_count), 1)
    offset = row + (key_count - rows) - col
    same_doc = kid_ref[...] == qid_ref[...]
    base_live = (offset >= 0) & same_doc
    for kv in range(width // d):
        kv_head(win_ref, q_ref, g_ref, kv_refs, dq_ref, own_ref, cross_refs, offset, base_live,
                kv, width, group_size)


def kv_head(win_ref, q_ref, g_ref, kv_refs, dq_ref, own_ref, cross_refs, offset, base_live,
            kv, width, group_size):
    d = HEAD_DIMENSION
    pieces = len(kv_refs)
    piece_rows = kv_refs[0].shape[0]
    keys = [ref[:, kv * d : (kv + 1) * d] for ref in kv_refs]
    values = [ref[:, width + kv * d : width + (kv + 1) * d] for ref in kv_refs]
    key_acc = [jnp.zeros((piece_rows, d), jnp.float32) for _ in range(pieces)]
    value_acc = [jnp.zeros((piece_rows, d), jnp.float32) for _ in range(pieces)]
    for h in range(group_size):
        head = kv * group_size + h
        query = q_ref[:, head * d : (head + 1) * d]
        grad = g_ref[:, head * d : (head + 1) * d]
        scores = jnp.concatenate([_nt(query, key) for key in keys], axis=1) * score_scale
        live = base_live & (offset < win_ref[head])
        scores = jnp.where(live, scores, jnp.float32(-1e30))
        top = jnp.max(scores, axis=1, keepdims=True)
        prob = jnp.exp(scores - top)
        prob = prob / jnp.sum(prob, axis=1, keepdims=True)
        prob_low = prob.astype(jnp.bfloat16)
        attended = _nn(prob_low[:, :piece_rows], values[0])
        for p in range(1, pieces):
            attended = attended + _nn(prob_low[:, p * piece_rows : (p + 1) * piece_rows], values[p])
        attended = attended.astype(jnp.bfloat16).astype(jnp.float32)
        delta = jnp.sum(grad.astype(jnp.float32) * attended, axis=1, keepdims=True)
        dprob = jnp.concatenate([_nt(grad, value) for value in values], axis=1)
        dscore = (prob * (dprob - delta)).astype(jnp.bfloat16)
        query_acc = _nn(dscore[:, :piece_rows], keys[0])
        for p in range(1, pieces):
            query_acc = query_acc + _nn(dscore[:, p * piece_rows : (p + 1) * piece_rows], keys[p])
        dq_ref[:, head * d : (head + 1) * d] = (query_acc * score_scale).astype(dq_ref.dtype)
        for p in range(pieces):
            cols = slice(p * piece_rows, (p + 1) * piece_rows)
            key_acc[p] = key_acc[p] + _tn(dscore[:, cols], query)
            value_acc[p] = value_acc[p] + _tn(prob_low[:, cols], grad)
    for p in range(pieces):
        target = own_ref if p == pieces - 1 else cross_refs[p]
        target[:, kv * d : (kv + 1) * d] = (key_acc[p] * score_scale).astype(target.dtype)
        target[:, width + kv * d : width + (kv + 1) * d] = value_acc[p].astype(target.dtype)


def head_group_grads(windows, query_ids, key_ids, query, grad, kv_pieces):
    pieces = len(kv_pieces)
    rows = query.shape[0]
    piece_rows = kv_pieces[0].shape[0]
    group_width = query.shape[1]
    pair_width = kv_pieces[0].shape[1]
    group_size = 2 * group_width // pair_width
    vmem = pl.BlockSpec(memory_space=pltpu.VMEM)
    smem = pl.BlockSpec(memory_space=pltpu.SMEM)
    out_shape = (
        [jax.ShapeDtypeStruct((rows, group_width), jnp.bfloat16)]
        + [jax.ShapeDtypeStruct((piece_rows, pair_width), jnp.float32)]
        + [jax.ShapeDtypeStruct((piece_rows, pair_width), jnp.bfloat16)] * (pieces - 1)
    )
    kernel = functools.partial(attention_kernel, pieces=pieces, group_size=group_size)
    outs = pl.pallas_call(
        kernel,
        out_shape=out_shape,
        in_specs=[smem] + [vmem] * (4 + pieces),
        out_specs=[vmem] * (pieces + 1),
        name="attention_group",
    )(windows, query_ids, key_ids, query, grad, *kv_pieces)
    return outs[0], outs[1], outs[2:]


def passed_along(value, axis, steps):
    count = lax.axis_size(axis)
    initial, last = (max(0, -steps), min(count, count - steps))
    return lax.ppermute(value, axis, [(source, source + steps) for source in range(initial, last)])


def on_device(query_proj, key_proj, value_projection, grad_out, doc_ids, advantages, head_window):
    tok_rows = query_proj.shape[0]
    kv_heads = key_proj.shape[1] // HEAD_DIMENSION
    q_heads = query_proj.shape[1] // HEAD_DIMENSION
    group_size = q_heads // kv_heads
    blocks = WINDOW // tok_rows
    first_pos = lax.axis_index("ctx") * tok_rows
    doc_count = advantages.shape[0]
    matches = doc_ids[:, None] == jnp.arange(doc_count, dtype=jnp.int32)[None, :]
    token_weight = jnp.sum(jnp.where(matches, advantages[None, :], jnp.float32(0.0)), axis=1)
    grad_local = lax.all_to_all(grad_out, "tsp", split_axis=1, concat_axis=0, tiled=True)
    weighted = (token_weight[:, None] * grad_local.astype(jnp.float32)).astype(jnp.bfloat16)

    ids_earlier = [passed_along(doc_ids, "ctx", distance) for distance in range(blocks, 0, -1)]
    key_ids = jnp.concatenate(ids_earlier + [doc_ids], axis=0)
    key_pos = first_pos - blocks * tok_rows + jnp.arange(key_ids.shape[0], dtype=jnp.int32)
    key_ids = jnp.where(key_pos >= 0, key_ids, jnp.int32(-1))[None, :]
    query_ids = doc_ids[:, None]

    chunk_heads = min(KV_PER_CHUNK, kv_heads)
    chunk_count = kv_heads // chunk_heads
    chunk_width = chunk_heads * HEAD_DIMENSION
    query_width = group_size * chunk_width

    query_pieces, key_pieces, value_pieces = [], [], []
    previous = None
    for chunk in range(chunk_count):
        cols = slice(chunk * chunk_width, (chunk + 1) * chunk_width)
        qcols = slice(chunk * query_width, (chunk + 1) * query_width)
        paired = jnp.concatenate([key_proj[:, cols], value_projection[:, cols]], axis=1)
        if previous is not None:
            paired, _ = lax.optimization_barrier((paired, previous))
        earlier = [passed_along(paired, "ctx", distance) for distance in range(blocks, 0, -1)]
        previous = earlier
        query_part, own_part, cross_parts = head_group_grads(
            head_window[chunk * group_size * chunk_heads : (chunk + 1) * group_size * chunk_heads],
            query_ids,
            key_ids,
            query_proj[:, qcols],
            weighted[:, qcols],
            earlier + [paired],
        )
        query_pieces.append(query_part)
        summed = own_part
        for index, piece in enumerate(cross_parts):
            arrived = passed_along(piece, "ctx", index - blocks)
            summed = summed + arrived.astype(jnp.float32)
        key_pieces.append(summed[:, :chunk_width])
        value_pieces.append(summed[:, chunk_width:])
    query_grad = jnp.concatenate(query_pieces, axis=1)
    key_grad = jnp.concatenate(key_pieces, axis=1).astype(jnp.bfloat16)
    value_grad = jnp.concatenate(value_pieces, axis=1).astype(jnp.bfloat16)
    return (query_grad, key_grad, value_grad)


def solution(mesh):
    in_specs = (
        P(("group", "ctx"), "tsp"),
        P(("group", "ctx"), "tsp"),
        P(("group", "ctx"), "tsp"),
        P(("group", "ctx", "tsp"), None),
        P(("group", "ctx")),
        P("group"),
        P("tsp"),
    )
    out_specs = (P(("group", "ctx"), "tsp"), P(("group", "ctx"), "tsp"), P(("group", "ctx"), "tsp"))
    return jax.shard_map(
        on_device, mesh=mesh, in_specs=in_specs, out_specs=out_specs, check_vma=False
    )
```

time: 203 us -> 152 us (0.75)
  the two profiles are of different devices: /device:TPU:8 before, /device:TPU:14 now
where the time goes in v2:
time: 152 us
  waiting for transfers between devices  96.9 us (64%)
  starting transfers between devices  29.4 us (19%)
  Pallas kernels  16.1 us (11%)
  local copies, waits for them, and re-layouts  5.33 us (4%)
  other arithmetic  3.31 us (2%)
    ppermute x12, waiting for transfers between devices, passed_along(): lax.ppermute(value, axis, [(source, source + steps) for source in range(i...  96.9 us
    ppermute x12, starting transfers between devices, passed_along(): lax.ppermute(value, axis, [(source, source + steps) for source in range(i...  25.8 us
    pallas_call x1, Pallas kernels, head_group_grads(): pl.pallas_call(kernel, out_shape=out_shape, in_specs=[smem] + [vmem] * (4...  16.1 us
    all_to_all x1, starting transfers between devices, on_device(): lax.all_to_all(grad_out, 'tsp', split_axis=1, concat_axis=0, tiled=True)  3.62 us
  transfers between devices with their start and end apart: 13, of which 8 were waited for; matrix products, arithmetic and copies ran while one was open for 3% of the time, Pallas kernels for 0%

profile of v2, /device:TPU:14, one launch (start us, length us, event | category | flops | bytes accessed | tf_op | source)
XLA Modules:
  0.0 151.9 jit_solution(4695413729797246148)
XLA Ops:
  0.6 3.5 %collective-permute-start.3 = (s32[256]{0:T(256)}, s32[256]{0:T(256)S(1)}, u32[]{:S(2)}, u32[]{:S(2)}) collective-permute-start(s32[256]{0:T(256)} %param.11), channel_id=1, source_target_pairs={{0,2},{2,4},{4,6},{6,8},{8,10},{10,12},{12,14},{1,3},{3,5},{5,7},{... | collective-permute-start | bytes 3080 | tf_op jit(solution)/shard_map/ppermute | solution.py:116
  4.1 3.5 %collective-permute-start.2 = (s32[256]{0:T(256)}, s32[256]{0:T(256)S(1)}, u32[]{:S(2)}, u32[]{:S(2)}) collective-permute-start(s32[256]{0:T(256)} %param.11), channel_id=1, source_target_pairs={{0,4},{2,6},{4,8},{6,10},{8,12},{10,14},{1,5},{3,7},{5,9},{7,11},{... | collective-permute-start | bytes 3080 | tf_op jit(solution)/shard_map/ppermute | solution.py:116
  7.6 2.2 %collective-permute-start.1 = (s32[256]{0:T(256)}, s32[256]{0:T(256)S(1)}, u32[]{:S(2)}, u32[]{:S(2)}) collective-permute-start(s32[256]{0:T(256)} %param.11), channel_id=1, source_target_pairs={{0,6},{2,8},{4,10},{6,12},{8,14},{1,7},{3,9},{5,11},{7,13},{9,15},... | collective-permute-start | bytes 3080 | tf_op jit(solution)/shard_map/ppermute | solution.py:116
  9.8 1.3 collective-permute-start
  11.1 1.9 %copy.17 = bf16[16,2,8,1024]{3,2,0,1:T(8,128)(2,1)} copy(bf16[16,2,8,1024]{3,2,1,0:T(8,128)(2,1)} %bitcast.16) | data formatting | bytes 1048576 | tf_op jit(solution)/shard_map/all_to_all | solution.py:129
  13.0 0.0 copy-start.5
  13.0 3.6 %all-to-all-start = ((bf16[128,2,1024]{2,0,1:T(8,128)(2,1)}), bf16[128,2,1024]{2,0,1:T(8,128)(2,1)S(1)}, u32[]{:S(2)}, u32[]{:S(2)}) async-start(bf16[128,2,1024]{2,0,1:T(8,128)(2,1)} %bitcast.15), calls=%async_computation | async-start | bytes 1048576 | tf_op jit(solution)/shard_map/all_to_all | solution.py:129
  16.6 0.0 copy-done.5
  16.6 0.0 copy-start.6
  16.7 0.9 copy-done.6
  17.6 0.0 copy-start.7
  17.6 0.0 copy-start.8
  17.6 0.0 copy-start
  17.6 3.1 %collective-permute-start.7 = (bf16[256,1024]{1,0:T(8,128)(2,1)S(1)}, bf16[256,1024]{1,0:T(8,128)(2,1)S(1)}, u32[]{:S(2)}, u32[]{:S(2)}) collective-permute-start(bf16[256,1024]{1,0:T(8,128)(2,1)S(1)} %constant_dynamic-update-slice_fusion.5.rest_4_), channel_id=1, source_target_pairs={{0,2},{2,4},{4,6},{6,8},{8,10},{10,12},{12,14},{1,3},{3,5},{5,7},{... | collective-permute-start | bytes 1572872 | tf_op jit(solution)/shard_map/ppermute | solution.py:116
  20.7 0.0 copy-done.7
  20.7 0.0 copy-done.8
  20.8 0.1 select_reduce_fusion
  20.8 0.0 all-to-all-done
  20.8 0.9 fusion.g_ref
  21.8 0.8 copy.14.qid_ref
  22.6 0.0 collective-permute-done
  22.6 1.9 %collective-permute-start.6 = (bf16[256,1024]{1,0:T(8,128)(2,1)S(1)}, bf16[256,1024]{1,0:T(8,128)(2,1)S(1)}, u32[]{:S(2)}, u32[]{:S(2)}) collective-permute-start(bf16[256,1024]{1,0:T(8,128)(2,1)S(1)} %constant_dynamic-update-slice_fusion.5.rest_4_), channel_id=1, source_target_pairs={{0,4},{2,6},{4,8},{6,10},{8,12},{10,14},{1,5},{3,7},{5,9},{7,11},{... | collective-permute-start | bytes 1572872 | tf_op jit(solution)/shard_map/ppermute | solution.py:116
  24.5 0.0 collective-permute-done.1
  24.5 1.9 %collective-permute-start.5 = (bf16[256,1024]{1,0:T(8,128)(2,1)S(1)}, bf16[256,1024]{1,0:T(8,128)(2,1)S(1)}, u32[]{:S(2)}, u32[]{:S(2)}) collective-permute-start(bf16[256,1024]{1,0:T(8,128)(2,1)S(1)} %constant_dynamic-update-slice_fusion.5.rest_4_), channel_id=1, source_target_pairs={{0,6},{2,8},{4,10},{6,12},{8,14},{1,7},{3,9},{5,11},{7,13},{9,15},... | collective-permute-start | bytes 1572872 | tf_op jit(solution)/shard_map/ppermute | solution.py:116
  26.5 0.0 collective-permute-done.2
  26.5 0.0 copy-done
  26.5 1.3 collective-permute-start.4
  27.8 0.0 collective-permute-done.3
  27.9 0.6 compare_select_fusion.kid_ref
  28.5 5.3 %collective-permute-done.7.rest_3_ = bf16[256,1024]{1,0:T(8,128)(2,1)S(1)} collective-permute-done((bf16[256,1024]{1,0:T(8,128)(2,1)S(1)}, bf16[256,1024]{1,0:T(8,128)(2,1)S(1)}, u32[]{:S(2)}, u32[]{:S(2)}) %collective-permute-start.7) | collective-permute-done | bytes 524320 | tf_op jit(solution)/shard_map/ppermute | solution.py:116
  33.8 0.0 copy-start.1
  33.8 12.3 %collective-permute-done.6.rest_2_ = bf16[256,1024]{1,0:T(8,128)(2,1)S(1)} collective-permute-done((bf16[256,1024]{1,0:T(8,128)(2,1)S(1)}, bf16[256,1024]{1,0:T(8,128)(2,1)S(1)}, u32[]{:S(2)}, u32[]{:S(2)}) %collective-permute-start.6) | collective-permute-done | bytes 524320 | tf_op jit(solution)/shard_map/ppermute | solution.py:116
  46.2 0.0 copy-start.2
  46.2 31.8 %collective-permute-done.5.rest_1_ = bf16[256,1024]{1,0:T(8,128)(2,1)S(1)} collective-permute-done((bf16[256,1024]{1,0:T(8,128)(2,1)S(1)}, bf16[256,1024]{1,0:T(8,128)(2,1)S(1)}, u32[]{:S(2)}, u32[]{:S(2)}) %collective-permute-start.5) | collective-permute-done | bytes 524320 | tf_op jit(solution)/shard_map/ppermute | solution.py:116
  78.0 0.0 copy-start.3
  78.0 10.7 %collective-permute-done.4.rest_0_ = bf16[256,1024]{1,0:T(8,128)(2,1)S(1)} collective-permute-done((bf16[256,1024]{1,0:T(8,128)(2,1)S(1)}, bf16[256,1024]{1,0:T(8,128)(2,1)S(1)}, u32[]{:S(2)}, u32[]{:S(2)}) %collective-permute-start.4) | collective-permute-done | bytes 524320 | tf_op jit(solution)/shard_map/ppermute | solution.py:116
  88.7 0.0 copy-done.1
  88.7 0.0 copy-done.2
  88.7 0.0 copy-done.3
  88.7 0.0 copy-start.4
  88.7 0.8 copy-done.4
  89.5 16.1 %attention_group.1 = (bf16[256,1024]{1,0:T(8,128)(2,1)}, f32[256,1024]{1,0:T(8,128)}, bf16[256,1024]{1,0:T(8,128)(2,1)}, bf16[256,1024]{1,0:T(8,128)(2,1)}, bf16...) custom-call(s32[8]{0:T(128)} %win_ref.1, s32[256,1]{1,0:T(8,128)} %copy.14.qid_ref, ...), custom_call_target="tpu_custom_call" | custom-call | tf_op jit(solution)/shard_map/attention_group/pallas_call | solution.py:103
  105.6 1.3 collective-permute-start.8
  106.9 1.9 %collective-permute-start.9 = (bf16[256,1024]{1,0:T(8,128)(2,1)}, bf16[256,1024]{1,0:T(8,128)(2,1)S(1)}, u32[]{:S(2)}, u32[]{:S(2)}) collective-permute-start(bf16[256,1024]{1,0:T(8,128)(2,1)} %get-tuple-element.12), channel_id=1, source_target_pairs={{6,0},{8,2},{10,4},{12,6},{14,8},{7,1},{9,3},{11,5},{13,7},{15,9},... | collective-permute-start | bytes 1572872 | tf_op jit(solution)/shard_map/ppermute | solution.py:116
  108.8 1.9 %collective-permute-start.10 = (bf16[256,1024]{1,0:T(8,128)(2,1)}, bf16[256,1024]{1,0:T(8,128)(2,1)S(1)}, u32[]{:S(2)}, u32[]{:S(2)}) collective-permute-start(bf16[256,1024]{1,0:T(8,128)(2,1)} %get-tuple-element.13), channel_id=1, source_target_pairs={{4,0},{6,2},{8,4},{10,6},{12,8},{14,10},{5,1},{7,3},{9,5},{11,7},{... | collective-permute-start | bytes 1572872 | tf_op jit(solution)/shard_map/ppermute | solution.py:116
  110.8 1.9 %collective-permute-start.11 = (bf16[256,1024]{1,0:T(8,128)(2,1)}, bf16[256,1024]{1,0:T(8,128)(2,1)S(1)}, u32[]{:S(2)}, u32[]{:S(2)}) collective-permute-start(bf16[256,1024]{1,0:T(8,128)(2,1)} %get-tuple-element.14), channel_id=1, source_target_pairs={{2,0},{4,2},{6,4},{8,6},{10,8},{12,10},{14,12},{3,1},{5,3},{7,5},{... | collective-permute-start | bytes 1572872 | tf_op jit(solution)/shard_map/ppermute | solution.py:116
  112.7 10.7 %collective-permute-done.8 = bf16[256,1024]{1,0:T(8,128)(2,1)S(1)} collective-permute-done((bf16[256,1024]{1,0:T(8,128)(2,1)}, bf16[256,1024]{1,0:T(8,128)(2,1)S(1)}, u32[]{:S(2)}, u32[]{:S(2)}) %collective-permute-start.8) | collective-permute-done | bytes 524320 | tf_op jit(solution)/shard_map/ppermute | solution.py:116
  123.4 2.2 %collective-permute-done.9 = bf16[256,1024]{1,0:T(8,128)(2,1)S(1)} collective-permute-done((bf16[256,1024]{1,0:T(8,128)(2,1)}, bf16[256,1024]{1,0:T(8,128)(2,1)S(1)}, u32[]{:S(2)}, u32[]{:S(2)}) %collective-permute-start.9) | collective-permute-done | bytes 524320 | tf_op jit(solution)/shard_map/ppermute | solution.py:116
  125.6 8.4 %collective-permute-done.10 = bf16[256,1024]{1,0:T(8,128)(2,1)S(1)} collective-permute-done((bf16[256,1024]{1,0:T(8,128)(2,1)}, bf16[256,1024]{1,0:T(8,128)(2,1)S(1)}, u32[]{:S(2)}, u32[]{:S(2)}) %collective-permute-start.10) | collective-permute-done | bytes 524320 | tf_op jit(solution)/shard_map/ppermute | solution.py:116
  134.0 15.3 %collective-permute-done.11 = bf16[256,1024]{1,0:T(8,128)(2,1)S(1)} collective-permute-done((bf16[256,1024]{1,0:T(8,128)(2,1)}, bf16[256,1024]{1,0:T(8,128)(2,1)S(1)}, u32[]{:S(2)}, u32[]{:S(2)}) %collective-permute-start.11) | collective-permute-done | bytes 524320 | tf_op jit(solution)/shard_map/ppermute | solution.py:116
  149.4 1.7 %add_convert_fusion = bf16[256,1024]{1,0:T(8,128)(2,1)S(1)} fusion(bf16[256,1024]{1,0:T(8,128)(2,1)S(1)} %collective-permute-done.11, bf16[256,1024]{1,0:T(8,128)(2,1)S(1)} %collective-permute-done.10, bf16[256,1024]{1,0:T(8,128)(2,1)S(1)} %collective-permute-done.9, f32[256,1024]{1,0:T(8,128)} %get-tuple-element.10, ...), kind=kLoop, calls=%fused_computation.2 | loop fusion | flops 2359296 | bytes 3670016 | tf_op jit(solution)/shard_map/convert.3
  151.0 0.8 fusion.1
  (7 shorter events, 0.1 us)
Async XLA Ops:
  0.6 27.2 %collective-permute-start.3 = (s32[256]{0:T(256)}, s32[256]{0:T(256)S(1)}, u32[]{:S(2)}, u32[]{:S(2)}) collective-permute-start(s32[256]{0:T(256)} %param.11), channel_id=1, source_target_pairs={{0,2},{2,4},{4,6},{6,8},{8,10},{10,12},{12,14},{1,3},{3,5},{5,7},{... | collective-permute-start | bytes 3080 | tf_op jit(solution)/shard_map/ppermute | solution.py:116
  4.1 22.4 %collective-permute-start.2 = (s32[256]{0:T(256)}, s32[256]{0:T(256)S(1)}, u32[]{:S(2)}, u32[]{:S(2)}) collective-permute-start(s32[256]{0:T(256)} %param.11), channel_id=1, source_target_pairs={{0,4},{2,6},{4,8},{6,10},{8,12},{10,14},{1,5},{3,7},{5,9},{7,11},{... | collective-permute-start | bytes 3080 | tf_op jit(solution)/shard_map/ppermute | solution.py:116
  7.6 16.9 %collective-permute-start.1 = (s32[256]{0:T(256)}, s32[256]{0:T(256)S(1)}, u32[]{:S(2)}, u32[]{:S(2)}) collective-permute-start(s32[256]{0:T(256)} %param.11), channel_id=1, source_target_pairs={{0,6},{2,8},{4,10},{6,12},{8,14},{1,7},{3,9},{5,11},{7,13},{9,15},... | collective-permute-start | bytes 3080 | tf_op jit(solution)/shard_map/ppermute | solution.py:116
  9.8 12.8 %collective-permute-start = (s32[256]{0:T(256)}, s32[256]{0:T(256)S(1)}, u32[]{:S(2)}, u32[]{:S(2)}) collective-permute-start(s32[256]{0:T(256)} %param.11), channel_id=1, source_target_pairs={{0,8},{2,10},{4,12},{6,14},{1,9},{3,11},{5,13},{7,15},{16,24},{18,... | collective-permute-start | bytes 3080 | tf_op jit(solution)/shard_map/ppermute | solution.py:116
  13.0 3.6 %copy-start.5 = (bf16[256,512]{1,0:T(8,128)(2,1)S(1)}, bf16[256,512]{1,0:T(8,128)(2,1)}, u32[]{:S(2)}) copy-start(bf16[256,512]{1,0:T(8,128)(2,1)} %param.8) | copy-start | bytes 786436
  13.0 7.9 %all-to-all-start = ((bf16[128,2,1024]{2,0,1:T(8,128)(2,1)}), bf16[128,2,1024]{2,0,1:T(8,128)(2,1)S(1)}, u32[]{:S(2)}, u32[]{:S(2)}) async-start(bf16[128,2,1024]{2,0,1:T(8,128)(2,1)} %bitcast.15), calls=%async_computation | async-start | bytes 1048576 | tf_op jit(solution)/shard_map/all_to_all | solution.py:129
  16.6 1.0 copy-start.6
  17.6 3.2 %copy-start.7 = (s32[256]{0:T(256)S(1)}, s32[256]{0:T(256)}, u32[]{:S(2)}) copy-start(s32[256]{0:T(256)} %param.11) | copy-start | bytes 3076
  17.6 3.2 %copy-start.8 = (f32[4]{0:T(128)S(1)}, f32[4]{0:T(128)}, u32[]{:S(2)}) copy-start(f32[4]{0:T(128)} %param.12) | copy-start | bytes 52
  17.6 8.9 %copy-start = (bf16[256,1024]{1,0:T(8,128)(2,1)}, bf16[256,1024]{1,0:T(8,128)(2,1)S(1)}, u32[]{:S(2)}) copy-start(bf16[256,1024]{1,0:T(8,128)(2,1)S(1)} %constant_dynamic-update-slice_fusion.5.rest_4_) | copy-start | bytes 1572868
  17.6 16.2 %collective-permute-start.7 = (bf16[256,1024]{1,0:T(8,128)(2,1)S(1)}, bf16[256,1024]{1,0:T(8,128)(2,1)S(1)}, u32[]{:S(2)}, u32[]{:S(2)}) collective-permute-start(bf16[256,1024]{1,0:T(8,128)(2,1)S(1)} %constant_dynamic-update-slice_fusion.5.rest_4_), channel_id=1, source_target_pairs={{0,2},{2,4},{4,6},{6,8},{8,10},{10,12},{12,14},{1,3},{3,5},{5,7},{... | collective-permute-start | bytes 1572872 | tf_op jit(solution)/shard_map/ppermute | solution.py:116
  22.6 23.6 %collective-permute-start.6 = (bf16[256,1024]{1,0:T(8,128)(2,1)S(1)}, bf16[256,1024]{1,0:T(8,128)(2,1)S(1)}, u32[]{:S(2)}, u32[]{:S(2)}) collective-permute-start(bf16[256,1024]{1,0:T(8,128)(2,1)S(1)} %constant_dynamic-update-slice_fusion.5.rest_4_), channel_id=1, source_target_pairs={{0,4},{2,6},{4,8},{6,10},{8,12},{10,14},{1,5},{3,7},{5,9},{7,11},{... | collective-permute-start | bytes 1572872 | tf_op jit(solution)/shard_map/ppermute | solution.py:116
  24.5 53.4 %collective-permute-start.5 = (bf16[256,1024]{1,0:T(8,128)(2,1)S(1)}, bf16[256,1024]{1,0:T(8,128)(2,1)S(1)}, u32[]{:S(2)}, u32[]{:S(2)}) collective-permute-start(bf16[256,1024]{1,0:T(8,128)(2,1)S(1)} %constant_dynamic-update-slice_fusion.5.rest_4_), channel_id=1, source_target_pairs={{0,6},{2,8},{4,10},{6,12},{8,14},{1,7},{3,9},{5,11},{7,13},{9,15},... | collective-permute-start | bytes 1572872 | tf_op jit(solution)/shard_map/ppermute | solution.py:116
  26.5 62.2 %collective-permute-start.4 = (bf16[256,1024]{1,0:T(8,128)(2,1)S(1)}, bf16[256,1024]{1,0:T(8,128)(2,1)S(1)}, u32[]{:S(2)}, u32[]{:S(2)}) collective-permute-start(bf16[256,1024]{1,0:T(8,128)(2,1)S(1)} %constant_dynamic-update-slice_fusion.5.rest_4_), channel_id=1, source_target_pairs={{0,8},{2,10},{4,12},{6,14},{1,9},{3,11},{5,13},{7,15},{16,24},{18,... | collective-permute-start | bytes 1572872 | tf_op jit(solution)/shard_map/ppermute | solution.py:116
  33.8 54.9 %copy-start.1 = (bf16[256,1024]{1,0:T(8,128)(2,1)}, bf16[256,1024]{1,0:T(8,128)(2,1)S(1)}, u32[]{:S(2)}) copy-start(bf16[256,1024]{1,0:T(8,128)(2,1)S(1)} %collective-permute-done.7.rest_3_) | copy-start | bytes 1572868
  46.2 42.5 %copy-start.2 = (bf16[256,1024]{1,0:T(8,128)(2,1)}, bf16[256,1024]{1,0:T(8,128)(2,1)S(1)}, u32[]{:S(2)}) copy-start(bf16[256,1024]{1,0:T(8,128)(2,1)S(1)} %collective-permute-done.6.rest_2_) | copy-start | bytes 1572868
  78.0 10.8 %copy-start.3 = (bf16[256,1024]{1,0:T(8,128)(2,1)}, bf16[256,1024]{1,0:T(8,128)(2,1)S(1)}, u32[]{:S(2)}) copy-start(bf16[256,1024]{1,0:T(8,128)(2,1)S(1)} %collective-permute-done.5.rest_1_) | copy-start | bytes 1572868
  88.7 0.8 copy-start.4
  105.6 17.8 %collective-permute-start.8 = (bf16[256,1024]{1,0:T(8,128)(2,1)}, bf16[256,1024]{1,0:T(8,128)(2,1)S(1)}, u32[]{:S(2)}, u32[]{:S(2)}) collective-permute-start(bf16[256,1024]{1,0:T(8,128)(2,1)} %get-tuple-element.11), channel_id=1, source_target_pairs={{8,0},{10,2},{12,4},{14,6},{9,1},{11,3},{13,5},{15,7},{24,16},{26,... | collective-permute-start | bytes 1572872 | tf_op jit(solution)/shard_map/ppermute | solution.py:116
  106.9 18.7 %collective-permute-start.9 = (bf16[256,1024]{1,0:T(8,128)(2,1)}, bf16[256,1024]{1,0:T(8,128)(2,1)S(1)}, u32[]{:S(2)}, u32[]{:S(2)}) collective-permute-start(bf16[256,1024]{1,0:T(8,128)(2,1)} %get-tuple-element.12), channel_id=1, source_target_pairs={{6,0},{8,2},{10,4},{12,6},{14,8},{7,1},{9,3},{11,5},{13,7},{15,9},... | collective-permute-start | bytes 1572872 | tf_op jit(solution)/shard_map/ppermute | solution.py:116
  108.8 25.2 %collective-permute-start.10 = (bf16[256,1024]{1,0:T(8,128)(2,1)}, bf16[256,1024]{1,0:T(8,128)(2,1)S(1)}, u32[]{:S(2)}, u32[]{:S(2)}) collective-permute-start(bf16[256,1024]{1,0:T(8,128)(2,1)} %get-tuple-element.13), channel_id=1, source_target_pairs={{4,0},{6,2},{8,4},{10,6},{12,8},{14,10},{5,1},{7,3},{9,5},{11,7},{... | collective-permute-start | bytes 1572872 | tf_op jit(solution)/shard_map/ppermute | solution.py:116
  110.8 38.6 %collective-permute-start.11 = (bf16[256,1024]{1,0:T(8,128)(2,1)}, bf16[256,1024]{1,0:T(8,128)(2,1)S(1)}, u32[]{:S(2)}, u32[]{:S(2)}) collective-permute-start(bf16[256,1024]{1,0:T(8,128)(2,1)} %get-tuple-element.14), channel_id=1, source_target_pairs={{2,0},{4,2},{6,4},{8,6},{10,8},{12,10},{14,12},{3,1},{5,3},{7,5},{... | collective-permute-start | bytes 1572872 | tf_op jit(solution)/shard_map/ppermute | solution.py:116

commit v3 on v2

--- a/solution.py
+++ b/solution.py
@@ -8,7 +8,7 @@
 
 HEAD_DIMENSION = 128
 WINDOW = 1024
-KV_PER_CHUNK = 4
+KV_PER_CHUNK = 2
 score_scale = 168.0 ** (-0.5)
 
 

time: 152 us -> 150 us (0.987)
  the two profiles are of different devices: /device:TPU:14 before, /device:TPU:11 now
where the time goes in v3:
time: 150 us; the launch traced here: 149 us
  starting transfers between devices  67.4 us (45%)
  waiting for transfers between devices  52.7 us (35%)
  Pallas kernels  17.5 us (12%)
  local copies, waits for them, and re-layouts  7.09 us (5%)
  other arithmetic  3.53 us (2%)
    ppermute x20, starting transfers between devices, passed_along(): lax.ppermute(value, axis, [(source, source + steps) for source in range(i...  62.6 us
    ppermute x20, waiting for transfers between devices, passed_along(): lax.ppermute(value, axis, [(source, source + steps) for source in range(i...  52.7 us
    pallas_call x2, Pallas kernels, head_group_grads(): pl.pallas_call(kernel, out_shape=out_shape, in_specs=[smem] + [vmem] * (4...  17.5 us
    all_to_all x1, starting transfers between devices, on_device(): lax.all_to_all(grad_out, 'tsp', split_axis=1, concat_axis=0, tiled=True)  4.85 us
  transfers between devices with their start and end apart: 21, of which 8 were waited for; matrix products, arithmetic and copies ran while one was open for 4% of the time, Pallas kernels for 12%

profile of v3, /device:TPU:11, one launch (start us, length us, event | category | flops | bytes accessed | tf_op | source)
XLA Modules:
  0.0 149.4 jit_solution(1640700487673226300)
XLA Ops:
  0.6 1.1 fusion.5
  1.8 0.0 copy-start.4
  1.8 4.4 %collective-permute-start.4 = (bf16[256,512]{1,0:T(8,128)(2,1)S(1)}, bf16[256,512]{1,0:T(8,128)(2,1)S(1)}, u32[]{:S(2)}, u32[]{:S(2)}) collective-permute-start(bf16[256,512]{1,0:T(8,128)(2,1)S(1)} %pad_maximum_fusion.1.rest_4_), channel_id=1, source_target_pairs={{0,8},{2,10},{4,12},{6,14},{1,9},{3,11},{5,13},{7,15},{16,24},{18,... | collective-permute-start | bytes 786440 | tf_op jit(solution)/shard_map/ppermute | solution.py:116
  6.2 1.9 %collective-permute-start.5 = (bf16[256,512]{1,0:T(8,128)(2,1)S(1)}, bf16[256,512]{1,0:T(8,128)(2,1)S(1)}, u32[]{:S(2)}, u32[]{:S(2)}) collective-permute-start(bf16[256,512]{1,0:T(8,128)(2,1)S(1)} %pad_maximum_fusion.1.rest_4_), channel_id=1, source_target_pairs={{0,6},{2,8},{4,10},{6,12},{8,14},{1,7},{3,9},{5,11},{7,13},{9,15},... | collective-permute-start | bytes 786440 | tf_op jit(solution)/shard_map/ppermute | solution.py:116
  8.1 1.9 %collective-permute-start.6 = (bf16[256,512]{1,0:T(8,128)(2,1)S(1)}, bf16[256,512]{1,0:T(8,128)(2,1)S(1)}, u32[]{:S(2)}, u32[]{:S(2)}) collective-permute-start(bf16[256,512]{1,0:T(8,128)(2,1)S(1)} %pad_maximum_fusion.1.rest_4_), channel_id=1, source_target_pairs={{0,4},{2,6},{4,8},{6,10},{8,12},{10,14},{1,5},{3,7},{5,9},{7,11},{... | collective-permute-start | bytes 786440 | tf_op jit(solution)/shard_map/ppermute | solution.py:116
  10.0 2.5 %collective-permute-start.7 = (bf16[256,512]{1,0:T(8,128)(2,1)S(1)}, bf16[256,512]{1,0:T(8,128)(2,1)S(1)}, u32[]{:S(2)}, u32[]{:S(2)}) collective-permute-start(bf16[256,512]{1,0:T(8,128)(2,1)S(1)} %pad_maximum_fusion.1.rest_4_), channel_id=1, source_target_pairs={{0,2},{2,4},{4,6},{6,8},{8,10},{10,12},{12,14},{1,3},{3,5},{5,7},{... | collective-permute-start | bytes 786440 | tf_op jit(solution)/shard_map/ppermute | solution.py:116
  12.5 0.8 copy.19
  13.3 4.8 %all-to-all-start = ((bf16[128,2,1024]{2,0,1:T(8,128)(2,1)}), bf16[128,2,1024]{2,0,1:T(8,128)(2,1)S(1)}, u32[]{:S(2)}, u32[]{:S(2)}) async-start(bf16[128,2,1024]{2,0,1:T(8,128)(2,1)} %bitcast.15), calls=%async_computation | async-start | bytes 1048576 | tf_op jit(solution)/shard_map/all_to_all | solution.py:129
  18.2 1.3 collective-permute-start
  19.5 0.1 select_reduce_fusion
  19.6 0.0 all-to-all-done
  19.6 0.2 fusion
  19.7 0.0 copy-start.5
  19.8 0.9 fusion.1
  20.6 0.4 copy-done.5
  21.0 0.8 fusion.2
  21.8 0.6 fusion.7
  22.4 0.8 copy.15.qid_ref
  23.2 17.0 %collective-permute-done = s32[256]{0:T(256)S(1)} collective-permute-done((s32[256]{0:T(256)S(1)}, s32[256]{0:T(256)S(1)}, u32[]{:S(2)}, u32[]{:S(2)}) %collective-permute-start) | collective-permute-done | bytes 1056 | tf_op jit(solution)/shard_map/ppermute | solution.py:116
  40.3 1.9 %collective-permute-start.1 = (s32[256]{0:T(256)S(1)}, s32[256]{0:T(256)S(1)}, u32[]{:S(2)}, u32[]{:S(2)}) collective-permute-start(s32[256]{0:T(256)S(1)} %copy-done.16), channel_id=1, source_target_pairs={{0,6},{2,8},{4,10},{6,12},{8,14},{1,7},{3,9},{5,11},{7,13},{9,15},... | collective-permute-start | bytes 3080 | tf_op jit(solution)/shard_map/ppermute | solution.py:116
  42.2 3.3 %collective-permute-done.1 = s32[256]{0:T(256)S(1)} collective-permute-done((s32[256]{0:T(256)S(1)}, s32[256]{0:T(256)S(1)}, u32[]{:S(2)}, u32[]{:S(2)}) %collective-permute-start.1) | collective-permute-done | bytes 1056 | tf_op jit(solution)/shard_map/ppermute | solution.py:116
  45.5 1.9 %collective-permute-start.2 = (s32[256]{0:T(256)S(1)}, s32[256]{0:T(256)S(1)}, u32[]{:S(2)}, u32[]{:S(2)}) collective-permute-start(s32[256]{0:T(256)S(1)} %copy-done.16), channel_id=1, source_target_pairs={{0,4},{2,6},{4,8},{6,10},{8,12},{10,14},{1,5},{3,7},{5,9},{7,11},{... | collective-permute-start | bytes 3080 | tf_op jit(solution)/shard_map/ppermute | solution.py:116
  47.4 2.4 %collective-permute-done.2 = s32[256]{0:T(256)S(1)} collective-permute-done((s32[256]{0:T(256)S(1)}, s32[256]{0:T(256)S(1)}, u32[]{:S(2)}, u32[]{:S(2)}) %collective-permute-start.2) | collective-permute-done | bytes 1056 | tf_op jit(solution)/shard_map/ppermute | solution.py:116
  49.8 3.3 %collective-permute-start.3 = (s32[256]{0:T(256)S(1)}, s32[256]{0:T(256)S(1)}, u32[]{:S(2)}, u32[]{:S(2)}) collective-permute-start(s32[256]{0:T(256)S(1)} %copy-done.16), channel_id=1, source_target_pairs={{0,2},{2,4},{4,6},{6,8},{8,10},{10,12},{12,14},{1,3},{3,5},{5,7},{... | collective-permute-start | bytes 3080 | tf_op jit(solution)/shard_map/ppermute | solution.py:116
  53.1 1.0 collective-permute-done.3
  54.1 0.0 collective-permute-done.4.rest_0_
  54.1 0.0 collective-permute-done.5.rest_1_
  54.1 0.0 collective-permute-done.6.rest_2_
  54.1 0.0 collective-permute-done.7.rest_3_
  54.2 3.3 %collective-permute-start.10 = (bf16[256,512]{1,0:T(8,128)(2,1)S(1)}, bf16[256,512]{1,0:T(8,128)(2,1)S(1)}, u32[]{:S(2)}, u32[]{:S(2)}) collective-permute-start(bf16[256,512]{1,0:T(8,128)(2,1)S(1)} %pad_maximum_fusion.2.rest_4_), channel_id=1, source_target_pairs={{0,4},{2,6},{4,8},{6,10},{8,12},{10,14},{1,5},{3,7},{5,9},{7,11},{... | collective-permute-start | bytes 786440 | tf_op jit(solution)/shard_map/ppermute | solution.py:116
  57.5 3.1 %collective-permute-start.11 = (bf16[256,512]{1,0:T(8,128)(2,1)S(1)}, bf16[256,512]{1,0:T(8,128)(2,1)S(1)}, u32[]{:S(2)}, u32[]{:S(2)}) collective-permute-start(bf16[256,512]{1,0:T(8,128)(2,1)S(1)} %pad_maximum_fusion.2.rest_4_), channel_id=1, source_target_pairs={{0,2},{2,4},{4,6},{6,8},{8,10},{10,12},{12,14},{1,3},{3,5},{5,7},{... | collective-permute-start | bytes 786440 | tf_op jit(solution)/shard_map/ppermute | solution.py:116
  60.6 1.3 collective-permute-start.8
  61.9 2.7 %collective-permute-start.9 = (bf16[256,512]{1,0:T(8,128)(2,1)S(1)}, bf16[256,512]{1,0:T(8,128)(2,1)S(1)}, u32[]{:S(2)}, u32[]{:S(2)}) collective-permute-start(bf16[256,512]{1,0:T(8,128)(2,1)S(1)} %pad_maximum_fusion.2.rest_4_), channel_id=1, source_target_pairs={{0,6},{2,8},{4,10},{6,12},{8,14},{1,7},{3,9},{5,11},{7,13},{9,15},... | collective-permute-start | bytes 786440 | tf_op jit(solution)/shard_map/ppermute | solution.py:116
  64.6 0.6 compare_select_fusion.kid_ref
  65.2 8.7 %attention_group.2 = (bf16[256,512]{1,0:T(8,128)(2,1)}, f32[256,512]{1,0:T(8,128)}, bf16[256,512]{1,0:T(8,128)(2,1)}, bf16[256,512]{1,0:T(8,128)(2,1)}, bf16[256...) custom-call(s32[4]{0:T(128)} %get-tuple-element.41.win_ref, s32[256,1]{1,0:T(8,128)} %copy.15.qid_ref, ...), custom_call_target="tpu_custom_call" | custom-call | tf_op jit(solution)/shard_map/attention_group/pallas_call | solution.py:103
  74.0 1.3 collective-permute-start.12
  75.3 0.0 collective-permute-done.10.rest_2_
  75.3 4.0 %collective-permute-start.13 = (bf16[256,512]{1,0:T(8,128)(2,1)}, bf16[256,512]{1,0:T(8,128)(2,1)S(1)}, u32[]{:S(2)}, u32[]{:S(2)}) collective-permute-start(bf16[256,512]{1,0:T(8,128)(2,1)} %get-tuple-element.21), channel_id=1, source_target_pairs={{6,0},{8,2},{10,4},{12,6},{14,8},{7,1},{9,3},{11,5},{13,7},{15,9},... | collective-permute-start | bytes 786440 | tf_op jit(solution)/shard_map/ppermute | solution.py:116
  79.3 0.0 collective-permute-done.11.rest_3_
  79.3 1.9 %collective-permute-start.14 = (bf16[256,512]{1,0:T(8,128)(2,1)}, bf16[256,512]{1,0:T(8,128)(2,1)S(1)}, u32[]{:S(2)}, u32[]{:S(2)}) collective-permute-start(bf16[256,512]{1,0:T(8,128)(2,1)} %get-tuple-element.22), channel_id=1, source_target_pairs={{4,0},{6,2},{8,4},{10,6},{12,8},{14,10},{5,1},{7,3},{9,5},{11,7},{... | collective-permute-start | bytes 786440 | tf_op jit(solution)/shard_map/ppermute | solution.py:116
  81.2 0.9 collective-permute-done.8.rest_0_
  82.1 2.1 %collective-permute-start.15 = (bf16[256,512]{1,0:T(8,128)(2,1)}, bf16[256,512]{1,0:T(8,128)(2,1)S(1)}, u32[]{:S(2)}, u32[]{:S(2)}) collective-permute-start(bf16[256,512]{1,0:T(8,128)(2,1)} %get-tuple-element.23), channel_id=1, source_target_pairs={{2,0},{4,2},{6,4},{8,6},{10,8},{12,10},{14,12},{3,1},{5,3},{7,5},{... | collective-permute-start | bytes 786440 | tf_op jit(solution)/shard_map/ppermute | solution.py:116
  84.2 3.7 %collective-permute-done.9.rest_1_ = bf16[256,512]{1,0:T(8,128)(2,1)S(1)} collective-permute-done((bf16[256,512]{1,0:T(8,128)(2,1)S(1)}, bf16[256,512]{1,0:T(8,128)(2,1)S(1)}, u32[]{:S(2)}, u32[]{:S(2)}) %collective-permute-start.9) | collective-permute-done | bytes 262176 | tf_op jit(solution)/shard_map/ppermute | solution.py:116
  87.9 0.7 copy-done.13
  88.6 8.8 %attention_group.3 = (bf16[256,512]{1,0:T(8,128)(2,1)}, f32[256,512]{1,0:T(8,128)}, bf16[256,512]{1,0:T(8,128)(2,1)}, bf16[256,512]{1,0:T(8,128)(2,1)}, bf16[256...) custom-call(s32[4]{0:T(128)} %get-tuple-element.42.win_ref, s32[256,1]{1,0:T(8,128)} %copy.15.qid_ref, ...), custom_call_target="tpu_custom_call" | custom-call | tf_op jit(solution)/shard_map/attention_group/pallas_call | solution.py:103
  97.3 1.3 collective-permute-start.16
  98.6 0.0 collective-permute-done.12
  98.6 1.9 %collective-permute-start.17 = (bf16[256,512]{1,0:T(8,128)(2,1)}, bf16[256,512]{1,0:T(8,128)(2,1)S(1)}, u32[]{:S(2)}, u32[]{:S(2)}) collective-permute-start(bf16[256,512]{1,0:T(8,128)(2,1)} %get-tuple-element.26), channel_id=1, source_target_pairs={{6,0},{8,2},{10,4},{12,6},{14,8},{7,1},{9,3},{11,5},{13,7},{15,9},... | collective-permute-start | bytes 786440 | tf_op jit(solution)/shard_map/ppermute | solution.py:116
  100.6 0.0 collective-permute-done.13
  100.6 5.2 %collective-permute-start.18 = (bf16[256,512]{1,0:T(8,128)(2,1)}, bf16[256,512]{1,0:T(8,128)(2,1)S(1)}, u32[]{:S(2)}, u32[]{:S(2)}) collective-permute-start(bf16[256,512]{1,0:T(8,128)(2,1)} %get-tuple-element.27), channel_id=1, source_target_pairs={{4,0},{6,2},{8,4},{10,6},{12,8},{14,10},{5,1},{7,3},{9,5},{11,7},{... | collective-permute-start | bytes 786440 | tf_op jit(solution)/shard_map/ppermute | solution.py:116
  105.8 0.0 collective-permute-done.14
  105.8 15.4 %collective-permute-start.19 = (bf16[256,512]{1,0:T(8,128)(2,1)}, bf16[256,512]{1,0:T(8,128)(2,1)S(1)}, u32[]{:S(2)}, u32[]{:S(2)}) collective-permute-start(bf16[256,512]{1,0:T(8,128)(2,1)} %get-tuple-element.28), channel_id=1, source_target_pairs={{2,0},{4,2},{6,4},{8,6},{10,8},{12,10},{14,12},{3,1},{5,3},{7,5},{... | collective-permute-start | bytes 786440 | tf_op jit(solution)/shard_map/ppermute | solution.py:116
  121.3 3.9 %collective-permute-done.15 = bf16[256,512]{1,0:T(8,128)(2,1)S(1)} collective-permute-done((bf16[256,512]{1,0:T(8,128)(2,1)}, bf16[256,512]{1,0:T(8,128)(2,1)S(1)}, u32[]{:S(2)}, u32[]{:S(2)}) %collective-permute-start.15) | collective-permute-done | bytes 262176 | tf_op jit(solution)/shard_map/ppermute | solution.py:116
  125.2 0.2 add_convert_fusion.1
  125.4 0.8 copy-done.14
  126.1 0.1 copy-done.15
  126.2 0.9 pad_maximum_fusion
  127.1 0.0 collective-permute-done.16
  127.1 0.0 collective-permute-done.17
  127.1 0.0 collective-permute-done.18
  127.1 20.6 %collective-permute-done.19 = bf16[256,512]{1,0:T(8,128)(2,1)S(1)} collective-permute-done((bf16[256,512]{1,0:T(8,128)(2,1)}, bf16[256,512]{1,0:T(8,128)(2,1)S(1)}, u32[]{:S(2)}, u32[]{:S(2)}) %collective-permute-start.19) | collective-permute-done | bytes 262176 | tf_op jit(solution)/shard_map/ppermute | solution.py:116
  147.7 0.2 add_convert_fusion
  147.9 0.7 pad_maximum_fusion.4
  148.6 0.7 pad_maximum_fusion.3
  (41 shorter events, 0.2 us)
Async XLA Ops:
  1.8 10.7 %copy-start.4 = (bf16[128,2048]{1,0:T(8,128)(2,1)S(1)}, bf16[128,2048]{1,0:T(8,128)(2,1)}, u32[]{:S(2)}) copy-start(bf16[128,2048]{1,0:T(8,128)(2,1)} %param.10) | copy-start | bytes 1572868
  1.8 11.5 %copy-start = (bf16[256,512]{1,0:T(8,128)(2,1)}, bf16[256,512]{1,0:T(8,128)(2,1)S(1)}, u32[]{:S(2)}) copy-start(bf16[256,512]{1,0:T(8,128)(2,1)S(1)} %pad_maximum_fusion.1.rest_4_) | copy-start | bytes 786436
  1.8 52.3 %collective-permute-start.4 = (bf16[256,512]{1,0:T(8,128)(2,1)S(1)}, bf16[256,512]{1,0:T(8,128)(2,1)S(1)}, u32[]{:S(2)}, u32[]{:S(2)}) collective-permute-start(bf16[256,512]{1,0:T(8,128)(2,1)S(1)} %pad_maximum_fusion.1.rest_4_), channel_id=1, source_target_pairs={{0,8},{2,10},{4,12},{6,14},{1,9},{3,11},{5,13},{7,15},{16,24},{18,... | collective-permute-start | bytes 786440 | tf_op jit(solution)/shard_map/ppermute | solution.py:116
  6.2 47.9 %collective-permute-start.5 = (bf16[256,512]{1,0:T(8,128)(2,1)S(1)}, bf16[256,512]{1,0:T(8,128)(2,1)S(1)}, u32[]{:S(2)}, u32[]{:S(2)}) collective-permute-start(bf16[256,512]{1,0:T(8,128)(2,1)S(1)} %pad_maximum_fusion.1.rest_4_), channel_id=1, source_target_pairs={{0,6},{2,8},{4,10},{6,12},{8,14},{1,7},{3,9},{5,11},{7,13},{9,15},... | collective-permute-start | bytes 786440 | tf_op jit(solution)/shard_map/ppermute | solution.py:116
  8.1 46.0 %collective-permute-start.6 = (bf16[256,512]{1,0:T(8,128)(2,1)S(1)}, bf16[256,512]{1,0:T(8,128)(2,1)S(1)}, u32[]{:S(2)}, u32[]{:S(2)}) collective-permute-start(bf16[256,512]{1,0:T(8,128)(2,1)S(1)} %pad_maximum_fusion.1.rest_4_), channel_id=1, source_target_pairs={{0,4},{2,6},{4,8},{6,10},{8,12},{10,14},{1,5},{3,7},{5,9},{7,11},{... | collective-permute-start | bytes 786440 | tf_op jit(solution)/shard_map/ppermute | solution.py:116
  10.0 44.1 %collective-permute-start.7 = (bf16[256,512]{1,0:T(8,128)(2,1)S(1)}, bf16[256,512]{1,0:T(8,128)(2,1)S(1)}, u32[]{:S(2)}, u32[]{:S(2)}) collective-permute-start(bf16[256,512]{1,0:T(8,128)(2,1)S(1)} %pad_maximum_fusion.1.rest_4_), channel_id=1, source_target_pairs={{0,2},{2,4},{4,6},{6,8},{8,10},{10,12},{12,14},{1,3},{3,5},{5,7},{... | collective-permute-start | bytes 786440 | tf_op jit(solution)/shard_map/ppermute | solution.py:116
  13.3 4.9 %copy-start.16 = (s32[256]{0:T(256)S(1)}, s32[256]{0:T(256)}, u32[]{:S(2)}) copy-start(s32[256]{0:T(256)} %param.11) | copy-start | bytes 3076
  13.3 6.1 %copy-start.18 = (f32[4]{0:T(128)S(1)}, f32[4]{0:T(128)}, u32[]{:S(2)}) copy-start(f32[4]{0:T(128)} %param.12) | copy-start | bytes 52
  13.3 6.2 %all-to-all-start = ((bf16[128,2,1024]{2,0,1:T(8,128)(2,1)}), bf16[128,2,1024]{2,0,1:T(8,128)(2,1)S(1)}, u32[]{:S(2)}, u32[]{:S(2)}) async-start(bf16[128,2,1024]{2,0,1:T(8,128)(2,1)} %bitcast.15), calls=%async_computation | async-start | bytes 1048576 | tf_op jit(solution)/shard_map/all_to_all | solution.py:129
  18.2 22.1 %collective-permute-start = (s32[256]{0:T(256)S(1)}, s32[256]{0:T(256)S(1)}, u32[]{:S(2)}, u32[]{:S(2)}) collective-permute-start(s32[256]{0:T(256)S(1)} %copy-done.16), channel_id=1, source_target_pairs={{0,8},{2,10},{4,12},{6,14},{1,9},{3,11},{5,13},{7,15},{16,24},{18,... | collective-permute-start | bytes 3080 | tf_op jit(solution)/shard_map/ppermute | solution.py:116
  19.7 1.2 copy-start.5
  21.0 0.8 copy-start.17
  22.4 51.5 %copy-start.1 = (bf16[256,512]{1,0:T(8,128)(2,1)}, bf16[256,512]{1,0:T(8,128)(2,1)S(1)}, u32[]{:S(2)}) copy-start(bf16[256,512]{1,0:T(8,128)(2,1)S(1)} %pad_maximum_fusion.2.rest_4_) | copy-start | bytes 786436
  40.3 5.2 %collective-permute-start.1 = (s32[256]{0:T(256)S(1)}, s32[256]{0:T(256)S(1)}, u32[]{:S(2)}, u32[]{:S(2)}) collective-permute-start(s32[256]{0:T(256)S(1)} %copy-done.16), channel_id=1, source_target_pairs={{0,6},{2,8},{4,10},{6,12},{8,14},{1,7},{3,9},{5,11},{7,13},{9,15},... | collective-permute-start | bytes 3080 | tf_op jit(solution)/shard_map/ppermute | solution.py:116
  45.5 4.3 %collective-permute-start.2 = (s32[256]{0:T(256)S(1)}, s32[256]{0:T(256)S(1)}, u32[]{:S(2)}, u32[]{:S(2)}) collective-permute-start(s32[256]{0:T(256)S(1)} %copy-done.16), channel_id=1, source_target_pairs={{0,4},{2,6},{4,8},{6,10},{8,12},{10,14},{1,5},{3,7},{5,9},{7,11},{... | collective-permute-start | bytes 3080 | tf_op jit(solution)/shard_map/ppermute | solution.py:116
  49.8 4.3 %collective-permute-start.3 = (s32[256]{0:T(256)S(1)}, s32[256]{0:T(256)S(1)}, u32[]{:S(2)}, u32[]{:S(2)}) collective-permute-start(s32[256]{0:T(256)S(1)} %copy-done.16), channel_id=1, source_target_pairs={{0,2},{2,4},{4,6},{6,8},{8,10},{10,12},{12,14},{1,3},{3,5},{5,7},{... | collective-permute-start | bytes 3080 | tf_op jit(solution)/shard_map/ppermute | solution.py:116
  54.1 11.1 %copy-start.6 = (bf16[256,512]{1,0:T(8,128)(2,1)}, bf16[256,512]{1,0:T(8,128)(2,1)S(1)}, u32[]{:S(2)}) copy-start(bf16[256,512]{1,0:T(8,128)(2,1)S(1)} %collective-permute-done.4.rest_0_) | copy-start | bytes 786436
  54.1 11.1 %copy-start.7 = (bf16[256,512]{1,0:T(8,128)(2,1)}, bf16[256,512]{1,0:T(8,128)(2,1)S(1)}, u32[]{:S(2)}) copy-start(bf16[256,512]{1,0:T(8,128)(2,1)S(1)} %collective-permute-done.5.rest_1_) | copy-start | bytes 786436
  54.1 11.1 %copy-start.8 = (bf16[256,512]{1,0:T(8,128)(2,1)}, bf16[256,512]{1,0:T(8,128)(2,1)S(1)}, u32[]{:S(2)}) copy-start(bf16[256,512]{1,0:T(8,128)(2,1)S(1)} %collective-permute-done.6.rest_2_) | copy-start | bytes 786436
  54.2 11.0 %copy-start.9 = (bf16[256,512]{1,0:T(8,128)(2,1)}, bf16[256,512]{1,0:T(8,128)(2,1)S(1)}, u32[]{:S(2)}) copy-start(bf16[256,512]{1,0:T(8,128)(2,1)S(1)} %collective-permute-done.7.rest_3_) | copy-start | bytes 786436
  54.2 21.1 %collective-permute-start.10 = (bf16[256,512]{1,0:T(8,128)(2,1)S(1)}, bf16[256,512]{1,0:T(8,128)(2,1)S(1)}, u32[]{:S(2)}, u32[]{:S(2)}) collective-permute-start(bf16[256,512]{1,0:T(8,128)(2,1)S(1)} %pad_maximum_fusion.2.rest_4_), channel_id=1, source_target_pairs={{0,4},{2,6},{4,8},{6,10},{8,12},{10,14},{1,5},{3,7},{5,9},{7,11},{... | collective-permute-start | bytes 786440 | tf_op jit(solution)/shard_map/ppermute | solution.py:116
  57.5 21.8 %collective-permute-start.11 = (bf16[256,512]{1,0:T(8,128)(2,1)S(1)}, bf16[256,512]{1,0:T(8,128)(2,1)S(1)}, u32[]{:S(2)}, u32[]{:S(2)}) collective-permute-start(bf16[256,512]{1,0:T(8,128)(2,1)S(1)} %pad_maximum_fusion.2.rest_4_), channel_id=1, source_target_pairs={{0,2},{2,4},{4,6},{6,8},{8,10},{10,12},{12,14},{1,3},{3,5},{5,7},{... | collective-permute-start | bytes 786440 | tf_op jit(solution)/shard_map/ppermute | solution.py:116
  60.6 21.5 %collective-permute-start.8 = (bf16[256,512]{1,0:T(8,128)(2,1)S(1)}, bf16[256,512]{1,0:T(8,128)(2,1)S(1)}, u32[]{:S(2)}, u32[]{:S(2)}) collective-permute-start(bf16[256,512]{1,0:T(8,128)(2,1)S(1)} %pad_maximum_fusion.2.rest_4_), channel_id=1, source_target_pairs={{0,8},{2,10},{4,12},{6,14},{1,9},{3,11},{5,13},{7,15},{16,24},{18,... | collective-permute-start | bytes 786440 | tf_op jit(solution)/shard_map/ppermute | solution.py:116
  61.9 26.0 %collective-permute-start.9 = (bf16[256,512]{1,0:T(8,128)(2,1)S(1)}, bf16[256,512]{1,0:T(8,128)(2,1)S(1)}, u32[]{:S(2)}, u32[]{:S(2)}) collective-permute-start(bf16[256,512]{1,0:T(8,128)(2,1)S(1)} %pad_maximum_fusion.2.rest_4_), channel_id=1, source_target_pairs={{0,6},{2,8},{4,10},{6,12},{8,14},{1,7},{3,9},{5,11},{7,13},{9,15},... | collective-permute-start | bytes 786440 | tf_op jit(solution)/shard_map/ppermute | solution.py:116
  74.0 24.7 %collective-permute-start.12 = (bf16[256,512]{1,0:T(8,128)(2,1)}, bf16[256,512]{1,0:T(8,128)(2,1)S(1)}, u32[]{:S(2)}, u32[]{:S(2)}) collective-permute-start(bf16[256,512]{1,0:T(8,128)(2,1)} %get-tuple-element.20), channel_id=1, source_target_pairs={{8,0},{10,2},{12,4},{14,6},{9,1},{11,3},{13,5},{15,7},{24,16},{26,... | collective-permute-start | bytes 786440 | tf_op jit(solution)/shard_map/ppermute | solution.py:116
  75.3 12.6 %copy-start.10 = (bf16[256,512]{1,0:T(8,128)(2,1)}, bf16[256,512]{1,0:T(8,128)(2,1)S(1)}, u32[]{:S(2)}) copy-start(bf16[256,512]{1,0:T(8,128)(2,1)S(1)} %collective-permute-done.10.rest_2_) | copy-start | bytes 786436
  75.3 25.3 %collective-permute-start.13 = (bf16[256,512]{1,0:T(8,128)(2,1)}, bf16[256,512]{1,0:T(8,128)(2,1)S(1)}, u32[]{:S(2)}, u32[]{:S(2)}) collective-permute-start(bf16[256,512]{1,0:T(8,128)(2,1)} %get-tuple-element.21), channel_id=1, source_target_pairs={{6,0},{8,2},{10,4},{12,6},{14,8},{7,1},{9,3},{11,5},{13,7},{15,9},... | collective-permute-start | bytes 786440 | tf_op jit(solution)/shard_map/ppermute | solution.py:116
  79.3 8.6 %copy-start.11 = (bf16[256,512]{1,0:T(8,128)(2,1)}, bf16[256,512]{1,0:T(8,128)(2,1)S(1)}, u32[]{:S(2)}) copy-start(bf16[256,512]{1,0:T(8,128)(2,1)S(1)} %collective-permute-done.11.rest_3_) | copy-start | bytes 786436
  79.3 26.5 %collective-permute-start.14 = (bf16[256,512]{1,0:T(8,128)(2,1)}, bf16[256,512]{1,0:T(8,128)(2,1)S(1)}, u32[]{:S(2)}, u32[]{:S(2)}) collective-permute-start(bf16[256,512]{1,0:T(8,128)(2,1)} %get-tuple-element.22), channel_id=1, source_target_pairs={{4,0},{6,2},{8,4},{10,6},{12,8},{14,10},{5,1},{7,3},{9,5},{11,7},{... | collective-permute-start | bytes 786440 | tf_op jit(solution)/shard_map/ppermute | solution.py:116
  82.1 5.8 %copy-start.12 = (bf16[256,512]{1,0:T(8,128)(2,1)}, bf16[256,512]{1,0:T(8,128)(2,1)S(1)}, u32[]{:S(2)}) copy-start(bf16[256,512]{1,0:T(8,128)(2,1)S(1)} %collective-permute-done.8.rest_0_) | copy-start | bytes 786436
  82.1 43.1 %collective-permute-start.15 = (bf16[256,512]{1,0:T(8,128)(2,1)}, bf16[256,512]{1,0:T(8,128)(2,1)S(1)}, u32[]{:S(2)}, u32[]{:S(2)}) collective-permute-start(bf16[256,512]{1,0:T(8,128)(2,1)} %get-tuple-element.23), channel_id=1, source_target_pairs={{2,0},{4,2},{6,4},{8,6},{10,8},{12,10},{14,12},{3,1},{5,3},{7,5},{... | collective-permute-start | bytes 786440 | tf_op jit(solution)/shard_map/ppermute | solution.py:116
  87.8 0.7 copy-start.13
  88.6 36.6 %copy-start.2 = (f32[256,512]{1,0:T(8,128)S(1)}, f32[256,512]{1,0:T(8,128)}, u32[]{:S(2)}) copy-start(f32[256,512]{1,0:T(8,128)} %get-tuple-element.19) | copy-start | bytes 1572868
  97.3 29.8 %collective-permute-start.16 = (bf16[256,512]{1,0:T(8,128)(2,1)}, bf16[256,512]{1,0:T(8,128)(2,1)S(1)}, u32[]{:S(2)}, u32[]{:S(2)}) collective-permute-start(bf16[256,512]{1,0:T(8,128)(2,1)} %get-tuple-element.25), channel_id=1, source_target_pairs={{8,0},{10,2},{12,4},{14,6},{9,1},{11,3},{13,5},{15,7},{24,16},{26,... | collective-permute-start | bytes 786440 | tf_op jit(solution)/shard_map/ppermute | solution.py:116
  98.6 28.5 %collective-permute-start.17 = (bf16[256,512]{1,0:T(8,128)(2,1)}, bf16[256,512]{1,0:T(8,128)(2,1)S(1)}, u32[]{:S(2)}, u32[]{:S(2)}) collective-permute-start(bf16[256,512]{1,0:T(8,128)(2,1)} %get-tuple-element.26), channel_id=1, source_target_pairs={{6,0},{8,2},{10,4},{12,6},{14,8},{7,1},{9,3},{11,5},{13,7},{15,9},... | collective-permute-start | bytes 786440 | tf_op jit(solution)/shard_map/ppermute | solution.py:116
  100.6 26.6 %collective-permute-start.18 = (bf16[256,512]{1,0:T(8,128)(2,1)}, bf16[256,512]{1,0:T(8,128)(2,1)S(1)}, u32[]{:S(2)}, u32[]{:S(2)}) collective-permute-start(bf16[256,512]{1,0:T(8,128)(2,1)} %get-tuple-element.27), channel_id=1, source_target_pairs={{4,0},{6,2},{8,4},{10,6},{12,8},{14,10},{5,1},{7,3},{9,5},{11,7},{... | collective-permute-start | bytes 786440 | tf_op jit(solution)/shard_map/ppermute | solution.py:116
  105.8 41.9 %collective-permute-start.19 = (bf16[256,512]{1,0:T(8,128)(2,1)}, bf16[256,512]{1,0:T(8,128)(2,1)S(1)}, u32[]{:S(2)}, u32[]{:S(2)}) collective-permute-start(bf16[256,512]{1,0:T(8,128)(2,1)} %get-tuple-element.28), channel_id=1, source_target_pairs={{2,0},{4,2},{6,4},{8,6},{10,8},{12,10},{14,12},{3,1},{5,3},{7,5},{... | collective-permute-start | bytes 786440 | tf_op jit(solution)/shard_map/ppermute | solution.py:116
  125.2 1.0 copy-start.14
  125.2 1.0 copy-start.15
  127.1 20.6 %copy-start.3 = (f32[256,512]{1,0:T(8,128)S(1)}, f32[256,512]{1,0:T(8,128)}, u32[]{:S(2)}) copy-start(f32[256,512]{1,0:T(8,128)} %get-tuple-element.24) | copy-start | bytes 1572868
